TPU v7x, 128 devices: a whole 4x4x4 slice. The times are simulated.
128 devices in a mesh: dp: 8 (over z, x_lo), ctx: 16 (over y, x_hi, core).
Axes of the slice: x: 4 (x_hi: 2, x_lo: 2; x = x_hi * 2 + x_lo), y: 4, z: 4, core: 2. Of those that a mesh axis runs over, the one named last changes fastest.
Arguments:
- tokens: bfloat16 [8, 262144, 128], P('dp', 'ctx'), may hold values from -6 to 6
- cotangent: bfloat16 [8, 262144, 128], P('dp', 'ctx'), may hold values from -6 to 6
- w_gate_value: bfloat16 [128, 256], replicated, may hold values from -0.5 to 0.5
- w_first: bfloat16 [512, 512], replicated, may hold values from -0.25 to 0.25
- w_second: bfloat16 [512, 512], replicated, may hold values from -0.25 to 0.25
- w_up: bfloat16 [128, 256], replicated, may hold values from -0.5 to 0.5
- w_down: bfloat16 [256, 128], replicated, may hold values from -0.375 to 0.375
Outputs:
- output: bfloat16 [8, 262144, 128], P('dp', 'ctx')
- grad_tokens: bfloat16 [8, 262144, 128], P('dp', 'ctx')
- grad_gate_value: float32 [128, 256], replicated
- grad_first: float32 [512, 512], replicated
- grad_second: float32 [512, 512], replicated
- grad_up: float32 [128, 256], replicated
- grad_down: float32 [256, 128], replicated
All inputs are finite; a program needn't handle non-finite values.
Results may differ from a plain program's by a relative error of at most 0.014.
Values may be sent and summed in bfloat16 or wider, within the bound.
No kernel may reach another device: no remote copies, remote signals or barrier semaphores. Data moves between devices by JAX's collectives and lax.ppermute only.
A program may use at most 256 MiB of HBM per device.

v0:
```python
import jax
import jax.numpy as jnp
from jax import lax
from jax.sharding import PartitionSpec as P


def silu_slope(pre):
    sigma = jax.nn.sigmoid(pre)
    return sigma * (1.0 + pre * (1.0 - sigma))


def body(tokens, cotangent, w_gate_value, w_first, w_second, w_up, w_down):
    f32 = jnp.float32
    bf16 = jnp.bfloat16
    seq_rows = tokens.shape[1]
    width = tokens.shape[2]
    block_size = w_first.shape[0]
    local_blocks = seq_rows // block_size
    seq_in = tokens[0]
    seq_cot = cotangent[0]
    projected = jnp.dot(seq_in, w_gate_value, preferred_element_type=f32)
    gate = jax.nn.sigmoid(projected[:, :width])
    values = projected[:, width:].astype(bf16)
    value_blocks = values.reshape(local_blocks, block_size, width)
    first = jnp.einsum("ijc,jk->ikc", value_blocks, w_first, preferred_element_type=f32).astype(
        bf16
    )
    first_mid = lax.all_to_all(first, "ctx", split_axis=1, concat_axis=0, tiled=True)
    mixed_mid = jnp.einsum("ikc,im->mkc", first_mid, w_second, preferred_element_type=f32).astype(
        bf16
    )
    mixed_blocks = lax.all_to_all(mixed_mid, "ctx", split_axis=0, concat_axis=1, tiled=True)
    mixed = mixed_blocks.reshape(seq_rows, width)
    hidden = (seq_in.astype(f32) + gate * mixed.astype(f32)).astype(bf16)
    pre = jnp.dot(hidden, w_up, preferred_element_type=f32)
    activated = jax.nn.silu(pre).astype(bf16)
    output = (hidden.astype(f32) + jnp.dot(activated, w_down, preferred_element_type=f32)).astype(
        bf16
    )
    grad_down = jnp.dot(activated.T, seq_cot, preferred_element_type=f32)
    d_act = (jnp.dot(seq_cot, w_down.T, preferred_element_type=f32) * silu_slope(pre)).astype(bf16)
    grad_up = jnp.dot(hidden.T, d_act, preferred_element_type=f32)
    d_hidden = (seq_cot.astype(f32) + jnp.dot(d_act, w_up.T, preferred_element_type=f32)).astype(
        bf16
    )
    d_mixed = (d_hidden.astype(f32) * gate).astype(bf16)
    d_gate = d_hidden.astype(f32) * mixed.astype(f32) * gate * (1.0 - gate)
    d_mixed_blocks = d_mixed.reshape(local_blocks, block_size, width)
    d_mixed_mid = lax.all_to_all(d_mixed_blocks, "ctx", split_axis=1, concat_axis=0, tiled=True)
    d_first_mid = jnp.einsum(
        "mkc,im->ikc", d_mixed_mid, w_second, preferred_element_type=f32
    ).astype(bf16)
    grad_second = jnp.einsum("ikc,mkc->im", first_mid, d_mixed_mid, preferred_element_type=f32)
    d_first = lax.all_to_all(d_first_mid, "ctx", split_axis=0, concat_axis=1, tiled=True)
    d_values = jnp.einsum("ikc,jk->ijc", d_first, w_first, preferred_element_type=f32).reshape(
        seq_rows, width
    )
    grad_first = jnp.einsum("ijc,ikc->jk", value_blocks, d_first, preferred_element_type=f32)
    d_projected = jnp.concatenate([d_gate, d_values], axis=1).astype(bf16)
    grad_gate_value = jnp.dot(seq_in.T, d_projected, preferred_element_type=f32)
    grad_tokens = (
        d_hidden.astype(f32) + jnp.dot(d_projected, w_gate_value.T, preferred_element_type=f32)
    ).astype(bf16)
    summed = lax.psum((grad_gate_value, grad_first, grad_second, grad_up, grad_down), ("dp", "ctx"))
    scale = float(seq_rows * lax.axis_size("ctx") * lax.axis_size("dp")) ** (-0.5)
    return (
        output[None],
        grad_tokens[None],
        summed[0] * scale,
        summed[1] * scale,
        summed[2] * scale,
        summed[3] * scale,
        summed[4] * scale,
    )


def solution(mesh):
    placed = (P("dp", "ctx", None), P("dp", "ctx", None), P(), P(), P(), P(), P())
    return jax.shard_map(
        body,
        mesh=mesh,
        in_specs=placed,
        out_specs=(P("dp", "ctx", None), P("dp", "ctx", None), P(), P(), P(), P(), P()),
        check_vma=False,
    )
```

profile of v0, /device:TPU:1, one launch (start us, length us, event | category | flops | bytes accessed | tf_op | source)
XLA Modules:
  0.0 547.1 jit_solution(15183325224199839789)
XLA Ops:
  11.8 5.7 %copy-done.1 = f32[16384,256]{1,0:T(8,128)} copy-done((f32[16384,256]{1,0:T(8,128)}, f32[16384,256]{1,0:T(8,128)S(1)}, u32[]{:S(2)}) %copy-start.1) | copy-done | bytes 16777240
  24.5 7.8 %copy.60 = bf16[32,512,128]{2,0,1:T(8,128)(2,1)} copy(bf16[32,512,128]{1,2,0:T(8,128)(2,1)} %convert_bitcast_fusion.4) | data formatting | bytes 8388608 | tf_op jit(solution)/shard_map/convert_element_type | solution.py:25
  32.3 58.9 %all_to_all.63 = bf16[32,512,128]{2,0,1:T(8,128)(2,1)S(1)} all-to-all(bf16[32,512,128]{2,0,1:T(8,128)(2,1)} %copy.60), channel_id=1, replica_groups=mesh['dp'=8,'ctx'=16] {'ctx'}, dimensions={1} | all-to-all | bytes 8388608 | tf_op jit(solution)/shard_map/all_to_all | solution.py:28
  95.0 5.8 %convert_bitcast_fusion.3 = bf16[512,32,128]{0,2,1:T(8,128)(2,1)} fusion(bf16[512,32,128]{2,1,0:T(8,128)(2,1)S(1)} %bitcast.97, bf16[512,512]{1,0:T(8,128)(2,1)S(1)} %copy-done), kind=kOutput, calls=%fused_computation.37 | convolution fusion | flops 2149580800 | bytes 8912896 | tf_op jit(solution)/shard_map/ikc,im->mkc/dot_general | solution.py:29
  100.8 7.8 %copy.64 = bf16[512,32,128]{2,1,0:T(8,128)(2,1)} copy(bf16[512,32,128]{0,2,1:T(8,128)(2,1)} %convert_bitcast_fusion.3) | data formatting | bytes 8388608 | tf_op jit(solution)/shard_map/convert_element_type | solution.py:29
  108.6 55.8 %all_to_all.64 = bf16[512,32,128]{2,1,0:T(8,128)(2,1)S(1)} all-to-all(bf16[512,32,128]{2,1,0:T(8,128)(2,1)} %copy.64), channel_id=1, replica_groups=mesh['dp'=8,'ctx'=16] {'ctx'}, dimensions={0} | all-to-all | bytes 8388608 | tf_op jit(solution)/shard_map/all_to_all | solution.py:32
  164.4 5.4 convert_bitcast_fusion
  169.8 8.2 %copy.65 = f32[32,16,32,128]{3,2,1,0:T(8,128)} copy(f32[32,16,32,128]{3,2,0,1:T(8,128)} %convert_bitcast_fusion) | data formatting | bytes 16777216 | tf_op jit(solution)/shard_map/convert_element_type | solution.py:34
  182.9 12.1 %multiply_convert_fusion = (bf16[16384,256]{1,0:T(8,128)(2,1)}, f32[16384,256]{1,0:T(8,128)}) fusion(bf16[16384,128]{1,0:T(8,128)(2,1)S(1)} %fusion.11, bf16[128,256]{1,0:T(8,128)(2,1)S(1)} %copy-done.17), kind=kOutput, calls=%fused_computation.11 | convolution fusion | flops 1094713344 | bytes 29425664 | tf_op jit(solution)/shard_map/dot_general | solution.py:35
  195.0 13.2 %fusion = bf16[16384,256]{1,0:T(8,128)(2,1)} fusion(bf16[256,128]{1,0:T(8,128)(2,1)S(1)} %copy-done.15, f32[16384,256]{1,0:T(8,128)} %get-tuple-element.43, bf16[1,16384,128]{2,1,0:T(8,128)(2,1)S(1)} %copy-done.8), kind=kOutput, calls=%fused_computation.1 | convolution fusion | flops 1111490560 | bytes 29425664 | tf_op jit(solution)/shard_map/dot_general | solution.py:41
  208.2 12.8 %fusion.14 = (bf16[16384,128]{1,0:T(8,128)(2,1)}, bf16[16384,128]{1,0:T(8,128)(2,1)}, f32[16384,128]{1,0:T(8,128)}) fusion(f32[32,16,32,128]{3,2,1,0:T(8,128)S(1)} %bitcast.93, f32[16384,256]{1,0:T(8,128)} %copy-done.1, bf16[16384,256]{1,0:T(8,128)(2,1)} %fusion, bf16[128,256]{1,0:T(8,128)(2,1)S(1)} %copy-done.17, bf16[1,16384,128]{2,1,0:T(8,128)(2,1)} %param.8), kind=kOutput, calls=%fused_computation.26 | convolution fusion | flops 1103101952 | bytes 46202880 | tf_op jit(solution)/shard_map/dot_general | solution.py:43
  221.0 4.9 copy.66
  225.9 54.3 %all_to_all.65 = bf16[32,512,128]{2,0,1:T(8,128)(2,1)S(1)} all-to-all(bf16[32,512,128]{2,0,1:T(8,128)(2,1)S(1)} %copy.66), channel_id=1, replica_groups=mesh['dp'=8,'ctx'=16] {'ctx'}, dimensions={1} | all-to-all | bytes 8388608 | tf_op jit(solution)/shard_map/all_to_all | solution.py:49
  284.0 6.4 %convert_bitcast_fusion.2 = bf16[512,32,128]{0,2,1:T(8,128)(2,1)} fusion(bf16[512,32,128]{2,1,0:T(8,128)(2,1)S(1)} %bitcast.103, bf16[512,512]{1,0:T(8,128)(2,1)S(1)} %copy-done), kind=kOutput, calls=%fused_computation.36 | convolution fusion | flops 2149580800 | bytes 8912896 | tf_op jit(solution)/shard_map/mkc,im->ikc/dot_general | solution.py:50
  290.4 7.9 %copy.70 = bf16[512,32,128]{2,1,0:T(8,128)(2,1)} copy(bf16[512,32,128]{0,2,1:T(8,128)(2,1)} %convert_bitcast_fusion.2) | data formatting | bytes 8388608 | tf_op jit(solution)/shard_map/convert_element_type | solution.py:52
  298.3 5.5 %all-to-all-start.3 = ((bf16[512,32,128]{2,1,0:T(8,128)(2,1)}), bf16[512,32,128]{2,1,0:T(8,128)(2,1)}, u32[]{:S(2)}, u32[]{:S(2)}) async-start(bf16[512,32,128]{2,1,0:T(8,128)(2,1)} %copy.70), calls=%async_computation.3 | async-start | bytes 8388608 | tf_op jit(solution)/shard_map/all_to_all | solution.py:54
  304.3 8.8 %fusion.47 = f32[128,256]{0,1:T(8,128)} fusion(bf16[16384,128]{1,0:T(8,128)(2,1)} %copy-done.2, bf16[16384,256]{1,0:T(8,128)(2,1)} %fusion), kind=kOutput, calls=%fused_computation.60 | convolution fusion | flops 1073741824 | bytes 12713984 | tf_op jit(solution)/shard_map/dot_general | solution.py:42
  313.1 6.6 %fusion.16 = f32[256,128]{1,0:T(8,128)} fusion(bf16[16384,256]{1,0:T(8,128)(2,1)} %get-tuple-element.42, bf16[1,16384,128]{2,1,0:T(8,128)(2,1)S(1)} %copy-done.9), kind=kOutput, calls=%fused_computation.29 | convolution fusion | flops 1073741824 | bytes 12713984 | tf_op jit(solution)/shard_map/dot_general | solution.py:40
  323.1 31.7 %all-to-all-done.3 = bf16[512,32,128]{2,1,0:T(8,128)(2,1)} async-done(((bf16[512,32,128]{2,1,0:T(8,128)(2,1)}), bf16[512,32,128]{2,1,0:T(8,128)(2,1)}, u32[]{:S(2)}, u32[]{:S(2)}) %all-to-all-start.3) | async-done | bytes 4194336 | tf_op jit(solution)/shard_map/all_to_all | solution.py:54
  366.4 6.4 %copy.73 = bf16[32,512,128]{2,1,0:T(8,128)(2,1)} copy(bf16[32,512,128]{1,2,0:T(8,128)(2,1)} %convert_bitcast_fusion.1) | data formatting | bytes 8388608 | tf_op jit(solution)/shard_map/ikc,jk->ijc/transpose | solution.py:55
  372.8 7.7 %fusion.38 = f32[128,256]{0,1:T(8,128)} fusion(bf16[1,16384,128]{2,1,0:T(8,128)(2,1)} %param.7, bf16[16384,128]{1,0:T(8,128)(2,1)} %bitcast.101, bf16[16384,128]{1,0:T(8,128)(2,1)} %get-tuple-element.40), kind=kOutput, calls=%fused_computation.48 | convolution fusion | flops 1090519040 | bytes 12713984 | tf_op jit(solution)/shard_map/dot_general | solution.py:60
  380.6 9.1 %fusion.6 = bf16[1,16384,128]{2,1,0:T(8,128)(2,1)} fusion(bf16[16384,256]{1,0:T(8,128)(2,1)} %get-tuple-element.42, bf16[256,128]{1,0:T(8,128)(2,1)S(1)} %copy-done.15, bf16[16384,128]{1,0:T(8,128)(2,1)} %copy-done.2), kind=kOutput, calls=%fused_computation.10 | convolution fusion | flops 1080033280 | bytes 16842752 | tf_op jit(solution)/shard_map/dot_general | solution.py:37
  389.7 6.2 %fusion.5 = bf16[1,16384,128]{2,1,0:T(8,128)(2,1)} fusion(f32[16384,128]{1,0:T(8,128)} %get-tuple-element.44, bf16[128,256]{1,0:T(8,128)(2,1)S(1)} %copy-done.16, bf16[16384,128]{1,0:T(8,128)(2,1)S(1)} %bitcast.102, bf16[16384,128]{1,0:T(8,128)(2,1)S(1)} %copy-done.18), kind=kOutput, calls=%fused_computation.9 | convolution fusion | flops 1094713344 | bytes 21037056 | tf_op jit(solution)/shard_map/dot_general | solution.py:62
  395.9 137.0 %all-reduce.3.cloned.1.call-done = (f32[128,256]{0,1:T(8,128)}, f32[512,512]{1,0:T(8,128)}, f32[512,512]{1,0:T(8,128)}, f32[128,256]{0,1:T(8,128)}, f32[256,128]{1,0:T(8,128)}) async-done(((f32[128,256]{0,1:T(8,128)}, f32[512,512]{1,0:T(8,128)}, f32[512,512]{1,0:T(8,128)}, f32[128,256]{0,1:T(8,128)}, f32[256,128]{1,0:T(8,128)}), (f32[128,256]{0,1:T(8,128)}, f32[512,512]{1,0:T(8,128)}, f32[512,512]{1,0:T(8,128)}, ...) | async-done | bytes 2490384 | tf_op jit(solution)/shard_map/psum | solution.py:64
  (68 shorter events, 46.5 us)
Async XLA Ops:
  7.2 87.8 %copy-start = (bf16[512,512]{1,0:T(8,128)(2,1)S(1)}, bf16[512,512]{1,0:T(8,128)(2,1)}, u32[]{:S(2)}) copy-start(bf16[512,512]{1,0:T(8,128)(2,1)} %param.11) | copy-start | bytes 1572868
  11.8 5.8 %copy-start.1 = (f32[16384,256]{1,0:T(8,128)}, f32[16384,256]{1,0:T(8,128)S(1)}, u32[]{:S(2)}) copy-start(f32[16384,256]{1,0:T(8,128)S(1)} %fusion.20) | copy-start | bytes 50331652
  17.5 2.6 copy-start.13
  108.6 69.5 %slice-start = ((s8[16777216]{0:T(1024)(128)(4,1)}), s8[4194304]{0:T(1024)(128)(4,1)S(1)}, s32[]{:S(2)}) async-start(s8[16777216]{0:T(1024)(128)(4,1)} %bitcast.90), calls=%async_computation.5 | async-start | bytes 8388608
  164.4 13.7 %slice-start.1 = ((s8[16777216]{0:T(1024)(128)(4,1)}), s8[4194304]{0:T(1024)(128)(4,1)S(1)}, s32[]{:S(2)}) async-start(s8[16777216]{0:T(1024)(128)(4,1)} %bitcast.90), calls=%async_computation.6 | async-start | bytes 8388608
  164.4 13.7 %slice-start.2 = ((s8[16777216]{0:T(1024)(128)(4,1)}), s8[4194304]{0:T(1024)(128)(4,1)S(1)}, s32[]{:S(2)}) async-start(s8[16777216]{0:T(1024)(128)(4,1)} %bitcast.90), calls=%async_computation.7 | async-start | bytes 8388608
  169.8 8.3 %slice-start.3 = ((s8[16777216]{0:T(1024)(128)(4,1)}), s8[4194304]{0:T(1024)(128)(4,1)S(1)}, s32[]{:S(2)}) async-start(s8[16777216]{0:T(1024)(128)(4,1)} %bitcast.90), calls=%async_computation.8 | async-start | bytes 8388608
  169.8 8.3 %copy-start.3 = (bf16[1,16384,128]{2,1,0:T(8,128)(2,1)S(1)}, bf16[1,16384,128]{2,1,0:T(8,128)(2,1)}, u32[]{:S(2)}) copy-start(bf16[1,16384,128]{2,1,0:T(8,128)(2,1)} %param.7) | copy-start | bytes 12582916
  178.1 4.7 copy-start.17
  182.8 12.2 %copy-start.2 = (bf16[16384,128]{1,0:T(8,128)(2,1)}, bf16[16384,128]{1,0:T(8,128)(2,1)S(1)}, u32[]{:S(2)}) copy-start(bf16[16384,128]{1,0:T(8,128)(2,1)S(1)} %fusion.11) | copy-start | bytes 12582916
  182.8 12.2 %copy-start.8 = (bf16[1,16384,128]{2,1,0:T(8,128)(2,1)S(1)}, bf16[1,16384,128]{2,1,0:T(8,128)(2,1)}, u32[]{:S(2)}) copy-start(bf16[1,16384,128]{2,1,0:T(8,128)(2,1)} %param.8) | copy-start | bytes 12582916
  182.9 12.2 %copy-start.15 = (bf16[256,128]{1,0:T(8,128)(2,1)S(1)}, bf16[256,128]{1,0:T(8,128)(2,1)}, u32[]{:S(2)}) copy-start(bf16[256,128]{1,0:T(8,128)(2,1)} %param.13) | copy-start | bytes 196612
  182.9 25.4 %slice-start.4 = ((s8[8388608]{0:T(1024)(128)(4,1)}), s8[4194304]{0:T(1024)(128)(4,1)S(1)}, s32[]{:S(2)}) async-start(s8[8388608]{0:T(1024)(128)(4,1)} %bitcast.92), calls=%async_computation.9 | async-start | bytes 8388608
  195.0 13.2 %slice-start.5 = ((s8[8388608]{0:T(1024)(128)(4,1)}), s8[4194304]{0:T(1024)(128)(4,1)S(1)}, s32[]{:S(2)}) async-start(s8[8388608]{0:T(1024)(128)(4,1)} %bitcast.92), calls=%async_computation.10 | async-start | bytes 8388608
  298.3 56.6 %all-to-all-start.3 = ((bf16[512,32,128]{2,1,0:T(8,128)(2,1)}), bf16[512,32,128]{2,1,0:T(8,128)(2,1)}, u32[]{:S(2)}, u32[]{:S(2)}) async-start(bf16[512,32,128]{2,1,0:T(8,128)(2,1)} %copy.70), calls=%async_computation.3 | async-start | bytes 8388608 | tf_op jit(solution)/shard_map/all_to_all | solution.py:54
  303.8 229.1 %all-reduce.3.cloned.1.call-start = ((), (), s32[]{:S(2)}) async-start(), calls=%async_computation.4 | async-start | bytes 4980736 | tf_op jit(solution)/shard_map/psum | solution.py:64
  304.3 8.8 %copy-start.9 = (bf16[1,16384,128]{2,1,0:T(8,128)(2,1)S(1)}, bf16[1,16384,128]{2,1,0:T(8,128)(2,1)}, u32[]{:S(2)}) copy-start(bf16[1,16384,128]{2,1,0:T(8,128)(2,1)} %param.8) | copy-start | bytes 12582916
  313.1 6.6 %copy-start.7 = (bf16[16,32,32,128]{3,2,1,0:T(8,128)(2,1)S(1)}, bf16[16,32,32,128]{3,2,1,0:T(8,128)(2,1)}, u32[]{:S(2)}) copy-start(bf16[16,32,32,128]{3,2,1,0:T(8,128)(2,1)} %copy-done.6) | copy-start | bytes 12582916
  313.1 6.6 %copy-start.12 = (bf16[16,32,32,128]{3,2,1,0:T(8,128)(2,1)S(1)}, bf16[16,32,32,128]{3,2,1,0:T(8,128)(2,1)}, u32[]{:S(2)}) copy-start(bf16[16,32,32,128]{3,2,1,0:T(8,128)(2,1)} %copy-done.11) | copy-start | bytes 12582916
  354.8 3.6 copy-start.5
  358.4 3.3 copy-start.14
  380.6 9.1 %copy-start.10 = (bf16[32,512,128]{2,1,0:T(8,128)(2,1)S(1)}, bf16[32,512,128]{2,1,0:T(8,128)(2,1)}, u32[]{:S(2)}) copy-start(bf16[32,512,128]{2,1,0:T(8,128)(2,1)} %copy.73) | copy-start | bytes 12582916
  380.6 9.1 %copy-start.16 = (bf16[128,256]{1,0:T(8,128)(2,1)S(1)}, bf16[128,256]{1,0:T(8,128)(2,1)}, u32[]{:S(2)}) copy-start(bf16[128,256]{1,0:T(8,128)(2,1)} %param.9) | copy-start | bytes 196612
  380.6 9.1 %copy-start.18 = (bf16[16384,128]{1,0:T(8,128)(2,1)S(1)}, bf16[16384,128]{1,0:T(8,128)(2,1)}, u32[]{:S(2)}) copy-start(bf16[16384,128]{1,0:T(8,128)(2,1)} %get-tuple-element.40) | copy-start | bytes 12582916
  (3 other events, 6.0 us)
Sparse Core Ops, SparseCore 0:
  380.7 152.1 all-reduce.2
where the time goes:
time: 556 us; the launch traced here: 547 us
  blocking collectives  169 us (30%)
  waiting for transfers between devices  169 us (30%)
  matrix products  109 us (20%)
  local copies, waits for them, and re-layouts  64.1 us (12%)
  other arithmetic  15.8 us (3%)
  between operations  14.5 us (3%)
  starting transfers between devices  5.98 us (1%)
    psum x1, waiting for transfers between devices, body(): lax.psum((grad_gate_value, grad_first, grad_second, grad_up, grad_down),...  137 us
    all_to_all x1, blocking collectives, body(): lax.all_to_all(first, 'ctx', split_axis=1, concat_axis=0, tiled=True)  58.9 us
    all_to_all x1, blocking collectives, body(): lax.all_to_all(mixed_mid, 'ctx', split_axis=0, concat_axis=1, tiled=True)  55.8 us
    all_to_all x1, blocking collectives, body(): lax.all_to_all(d_mixed_blocks, 'ctx', split_axis=1, concat_axis=0, tiled=...  54.3 us
    all_to_all x1, waiting for transfers between devices, body(): lax.all_to_all(d_first_mid, 'ctx', split_axis=0, concat_axis=1, tiled=True)  31.7 us
    unnamed x52, local copies, waits for them, and re-layouts  13.3 us
    dot_general x1, matrix products, body(): jnp.dot(seq_cot, w_down.T, preferred_element_type=f32) * silu_slope(pre)  13.2 us
    dot_general x1, matrix products, body(): jnp.dot(d_act, w_up.T, preferred_element_type=f32)  12.8 us
  transfers between devices with their start and end apart: 2, of which 2 were waited for; matrix products, arithmetic and copies ran while one was open for 6% of the time, Pallas kernels for 0%

commit v1 on v0

v1 whole, which is shorter than its diff:
```python
import jax
import jax.numpy as jnp
from jax import lax
from jax.sharding import PartitionSpec as P

CHUNKS = 1


def silu_slope(pre):
    sigma = jax.nn.sigmoid(pre)
    return sigma * (1.0 + pre * (1.0 - sigma))


def a2a(x, axis):
    return lax.all_to_all(x, axis, 0, 0, tiled=True)


def all_reduce_a2a(flat):
    n_ctx = lax.axis_size("ctx")
    n_dp = lax.axis_size("dp")
    rows, width = flat.shape
    part = rows // n_ctx
    piece = part // n_dp
    a = a2a(flat.reshape(n_ctx, part, width), "ctx").sum(0)
    b = a2a(a.reshape(n_dp, piece, width), "dp").sum(0)
    c = a2a(jnp.broadcast_to(b[None], (n_dp, piece, width)), "dp").reshape(part, width)
    d = a2a(jnp.broadcast_to(c[None], (n_ctx, part, width)), "ctx").reshape(rows, width)
    return d


def body(tokens, cotangent, w_gate_value, w_first, w_second, w_up, w_down):
    f32 = jnp.float32
    bf16 = jnp.bfloat16
    n_ctx = lax.axis_size("ctx")
    n_dp = lax.axis_size("dp")
    seq_rows = tokens.shape[1]
    width = tokens.shape[2]
    block_size = w_first.shape[0]
    local_blocks = seq_rows // block_size
    all_blocks = w_second.shape[0]
    per_dev = block_size // n_ctx
    q_n = CHUNKS
    r_n = per_dev // q_n
    seq_in = tokens[0]
    seq_cot = cotangent[0]
    projected = jnp.dot(seq_in, w_gate_value, preferred_element_type=f32)
    gate = jax.nn.sigmoid(projected[:, :width])
    values = projected[:, width:].astype(bf16)
    value_blocks = values.reshape(local_blocks, block_size, width)
    wf = w_first.reshape(block_size, n_ctx, q_n, r_n)
    x5 = seq_in.reshape(local_blocks, n_ctx, q_n, r_n, width)
    c5 = seq_cot.reshape(local_blocks, n_ctx, q_n, r_n, width)
    g5 = gate.reshape(local_blocks, n_ctx, q_n, r_n, width)

    grad_down = jnp.zeros((w_down.shape[0], width), f32)
    grad_up = jnp.zeros((width, w_up.shape[1]), f32)
    grad_second = jnp.zeros((all_blocks, all_blocks), f32)
    d_values = jnp.zeros((local_blocks, block_size, width), f32)
    outs, d_hiddens, d_gates, gf_parts = [], [], [], []
    for q in range(q_n):
        wf_q = wf[:, :, q, :]
        first_q = jnp.einsum("ijc,jdr->dirc", value_blocks, wf_q, preferred_element_type=f32).astype(bf16)
        first_mid = a2a(first_q, "ctx").reshape(all_blocks, r_n, width)
        mixed_mid = jnp.einsum("ikc,im->mkc", first_mid, w_second, preferred_element_type=f32).astype(bf16)
        mixed = a2a(mixed_mid.reshape(n_ctx, local_blocks, r_n, width), "ctx")
        mixed = mixed.reshape(-1, width)
        xq = x5[:, :, q].transpose(1, 0, 2, 3).reshape(-1, width)
        cq = c5[:, :, q].transpose(1, 0, 2, 3).reshape(-1, width)
        gq = g5[:, :, q].transpose(1, 0, 2, 3).reshape(-1, width)
        mixed32 = mixed.astype(f32)
        hidden = (xq.astype(f32) + gq * mixed32).astype(bf16)
        pre = jnp.dot(hidden, w_up, preferred_element_type=f32)
        activated = jax.nn.silu(pre).astype(bf16)
        out_q = (hidden.astype(f32) + jnp.dot(activated, w_down, preferred_element_type=f32)).astype(bf16)
        grad_down = grad_down + jnp.dot(activated.T, cq, preferred_element_type=f32)
        d_act = (jnp.dot(cq, w_down.T, preferred_element_type=f32) * silu_slope(pre)).astype(bf16)
        grad_up = grad_up + jnp.dot(hidden.T, d_act, preferred_element_type=f32)
        d_hidden = (cq.astype(f32) + jnp.dot(d_act, w_up.T, preferred_element_type=f32)).astype(bf16)
        d_mixed = (d_hidden.astype(f32) * gq).astype(bf16)
        d_gate = d_hidden.astype(f32) * mixed32 * gq * (1.0 - gq)
        d_mixed_mid = a2a(d_mixed.reshape(n_ctx, local_blocks, r_n, width), "ctx")
        d_mixed_mid = d_mixed_mid.reshape(all_blocks, r_n, width)
        d_first_mid = jnp.einsum("mkc,im->ikc", d_mixed_mid, w_second, preferred_element_type=f32).astype(bf16)
        grad_second = grad_second + jnp.einsum(
            "ikc,mkc->im", first_mid, d_mixed_mid, preferred_element_type=f32
        )
        d_first = a2a(d_first_mid.reshape(n_ctx, local_blocks, r_n, width), "ctx")
        d_values = d_values + jnp.einsum("dirc,jdr->ijc", d_first, wf_q, preferred_element_type=f32)
        gf_parts.append(jnp.einsum("ijc,dirc->jdr", value_blocks, d_first, preferred_element_type=f32))
        outs.append(out_q.reshape(n_ctx, local_blocks, r_n, width))
        d_hiddens.append(d_hidden.reshape(n_ctx, local_blocks, r_n, width))
        d_gates.append(d_gate.reshape(n_ctx, local_blocks, r_n, width))

    def rows_of(parts):
        return jnp.stack(parts, axis=2).transpose(1, 0, 2, 3, 4).reshape(seq_rows, width)

    output = rows_of(outs)
    d_hidden = rows_of(d_hiddens)
    d_gate = rows_of(d_gates)
    grad_first = jnp.stack(gf_parts, axis=2).reshape(block_size, block_size)
    d_projected = jnp.concatenate([d_gate, d_values.reshape(seq_rows, width)], axis=1).astype(bf16)
    grad_gate_value = jnp.dot(seq_in.T, d_projected, preferred_element_type=f32)
    grad_tokens = (
        d_hidden.astype(f32) + jnp.dot(d_projected, w_gate_value.T, preferred_element_type=f32)
    ).astype(bf16)

    grads = (grad_gate_value, grad_first, grad_second, grad_up, grad_down)
    lane = 128
    flat = jnp.concatenate([g.reshape(-1, lane) for g in grads], axis=0)
    summed = all_reduce_a2a(flat)
    scale = float(seq_rows * n_ctx * n_dp) ** (-0.5)
    summed = summed * scale
    results = []
    at = 0
    for g in grads:
        n = g.size // lane
        results.append(summed[at:at + n].reshape(g.shape))
        at += n
    return (output[None], grad_tokens[None], *results)


def solution(mesh):
    placed = (P("dp", "ctx", None), P("dp", "ctx", None), P(), P(), P(), P(), P())
    return jax.shard_map(
        body,
        mesh=mesh,
        in_specs=placed,
        out_specs=(P("dp", "ctx", None), P("dp", "ctx", None), P(), P(), P(), P(), P()),
        check_vma=False,
    )
```

time: 556 us -> 481 us (0.87)
  waiting for transfers between devices: 169 us -> 79 us
  local copies, waits for them, and re-layouts: 64.1 us -> 79.1 us
  starting transfers between devices: 5.98 us -> 19.4 us
  between operations: 14.5 us -> 1.41 us
    psum x1 -> x0, waiting for transfers between devices: 137 us -> none  [body(): lax.psum((grad_gate_value, grad_first, grad_second, grad_up, grad_down),...]
    all_to_all x1 -> x3, waiting for transfers between devices: 31.7 us -> 79 us  [a2a(): return lax.all_to_all(x, axis, 0, 0, tiled=True)]
    all_to_all x1 -> x3, starting transfers between devices: 5.54 us -> 19.4 us  [a2a(): return lax.all_to_all(x, axis, 0, 0, tiled=True)]
    another operation x0 -> x3, local copies, waits for them, and re-layouts: none -> 12.1 us  [the longest x1 5.59 us: rows_of(): jnp.stack(parts, axis=2).transpose(1, 0, 2, 3, 4).reshape(seq_rows, width)]
    transpose x1 -> x3, local copies, waits for them, and re-layouts: 6.43 us -> 13.9 us  [the longest x1 6.45 us: body(): jnp.einsum('dirc,jdr->ijc', d_first, wf_q, preferred_element_type=f32)]
    all_to_all x3 -> x0, local copies, waits for them, and re-layouts: 7.11 us -> none  [the longest x1 3.59 us: body(): lax.all_to_all(d_first_mid, 'ctx', split_axis=0, concat_axis=1, tiled=True)]
    convert_element_type x3 -> x4, local copies, waits for them, and re-layouts: 24 us -> 18 us  [the longest x1 7.94 us: body(): jnp.einsum('mkc,im->ikc', d_mixed_mid, w_second, preferred_element_type=f32)]
    all_to_all x3 -> x5, blocking collectives: 169 us -> 169 us  [a2a(): return lax.all_to_all(x, axis, 0, 0, tiled=True)]
  transfers between devices with their start and end apart: 2 -> 3, of which waited for: 2 -> 3; matrix products, arithmetic and copies ran while one was open for 6% -> 12% of each run, Pallas kernels for 0% -> 0%
where the time goes in v1:
time: 481 us; the launch traced here: 473 us
  blocking collectives  169 us (35%)
  matrix products  112 us (23%)
  local copies, waits for them, and re-layouts  79.1 us (16%)
  waiting for transfers between devices  79 us (16%)
  starting transfers between devices  19.4 us (4%)
  other arithmetic  12.5 us (3%)
    all_to_all x5, blocking collectives, a2a(): return lax.all_to_all(x, axis, 0, 0, tiled=True)  169 us
    all_to_all x3, waiting for transfers between devices, a2a(): return lax.all_to_all(x, axis, 0, 0, tiled=True)  79 us
    all_to_all x3, starting transfers between devices, a2a(): return lax.all_to_all(x, axis, 0, 0, tiled=True)  19.4 us
    dot_general x1, matrix products, body(): jnp.dot(d_act, w_up.T, preferred_element_type=f32)  15 us
    unnamed x41, local copies, waits for them, and re-layouts  13.5 us
    dot_general x1, matrix products, body(): jnp.dot(cq, w_down.T, preferred_element_type=f32) * silu_slope(pre)  13.3 us
    dot_general x1, matrix products, body(): pre = jnp.dot(hidden, w_up, preferred_element_type=f32)  12.1 us
  transfers between devices with their start and end apart: 3, of which 3 were waited for; matrix products, arithmetic and copies ran while one was open for 12% of the time, Pallas kernels for 0%

profile of v1, /device:TPU:1, one launch (start us, length us, event | category | flops | bytes accessed | tf_op | source)
XLA Modules:
  0.0 473.0 jit_solution(17374891396720226031)
XLA Ops:
  19.1 58.7 %all_to_all.40 = bf16[16,32,32,128]{3,2,1,0:T(8,128)(2,1)S(1)} all-to-all(bf16[16,32,32,128]{3,2,1,0:T(8,128)(2,1)S(1)} %copy.49), channel_id=1, replica_groups=mesh['dp'=8,'ctx'=16] {'ctx'}, dimensions={0} | all-to-all | bytes 8388608 | tf_op jit(solution)/shard_map/all_to_all | solution.py:15
  79.8 6.1 %convert_bitcast_fusion.1 = bf16[512,32,128]{0,2,1:T(8,128)(2,1)} fusion(bf16[512,32,128]{2,1,0:T(8,128)(2,1)S(1)} %bitcast.120, bf16[512,512]{1,0:T(8,128)(2,1)S(1)} %copy-done), kind=kOutput, calls=%fused_computation.35 | convolution fusion | flops 2149580800 | bytes 8912896 | tf_op jit(solution)/shard_map/ikc,im->mkc/dot_general | solution.py:64
  85.8 7.9 %copy.51 = bf16[512,32,128]{2,1,0:T(8,128)(2,1)} copy(bf16[512,32,128]{0,2,1:T(8,128)(2,1)} %convert_bitcast_fusion.1) | data formatting | bytes 8388608 | tf_op jit(solution)/shard_map/convert_element_type | solution.py:64
  93.7 6.1 %all-to-all-start.1 = ((bf16[16,32,32,128]{3,2,1,0:T(8,128)(2,1)}), bf16[16,32,32,128]{3,2,1,0:T(8,128)(2,1)}, u32[]{:S(2)}, u32[]{:S(2)}) async-start(bf16[16,32,32,128]{3,2,1,0:T(8,128)(2,1)} %bitcast.123), calls=%async_computation.1 | async-start | bytes 8388608 | tf_op jit(solution)/shard_map/all_to_all | solution.py:15
  116.3 34.5 %all-to-all-done.1 = bf16[16,32,32,128]{3,2,1,0:T(8,128)(2,1)} async-done(((bf16[16,32,32,128]{3,2,1,0:T(8,128)(2,1)}), bf16[16,32,32,128]{3,2,1,0:T(8,128)(2,1)}, u32[]{:S(2)}, u32[]{:S(2)}) %all-to-all-start.1) | async-done | bytes 4194336 | tf_op jit(solution)/shard_map/all_to_all | solution.py:15
  150.7 7.6 %fusion.7 = bf16[16384,128]{1,0:T(8,128)(2,1)S(1)} fusion(f32[32,16,32,128]{3,2,0,1:T(8,128)} %copy.46, f32[16,32,32,128]{3,2,1,0:T(8,128)} %copy.47, bf16[16,32,32,128]{3,2,1,0:T(8,128)(2,1)} %all-to-all-done.1), kind=kLoop, calls=%fused_computation.15 | loop fusion | flops 8388608 | bytes 25165824 | tf_op jit(solution)/shard_map/convert_element_type | solution.py:71
  158.4 12.1 %multiply_convert_fusion = (bf16[16384,256]{1,0:T(8,128)(2,1)}, f32[16384,256]{1,0:T(8,128)}) fusion(bf16[16384,128]{1,0:T(8,128)(2,1)S(1)} %fusion.7, bf16[128,256]{1,0:T(8,128)(2,1)S(1)} %copy-done.13), kind=kOutput, calls=%fused_computation.10 | convolution fusion | flops 1094713344 | bytes 29425664 | tf_op jit(solution)/shard_map/dot_general | solution.py:72
  170.6 13.3 %fusion = bf16[16384,256]{1,0:T(8,128)(2,1)} fusion(bf16[16384,128]{1,0:T(8,128)(2,1)S(1)} %bitcast.112, bf16[256,128]{1,0:T(8,128)(2,1)S(1)} %copy-done.14, f32[16384,256]{1,0:T(8,128)} %get-tuple-element.15), kind=kOutput, calls=%fused_computation.1 | convolution fusion | flops 1111490560 | bytes 29425664 | tf_op jit(solution)/shard_map/dot_general | solution.py:76
  183.9 15.0 %fusion.10 = (bf16[16384,128]{1,0:T(8,128)(2,1)}, bf16[16384,128]{1,0:T(8,128)(2,1)}, f32[16384,128]{1,0:T(8,128)}) fusion(f32[16,32,32,128]{3,2,1,0:T(8,128)S(1)} %bitcast.110, bf16[16,32,32,128]{3,2,1,0:T(8,128)(2,1)} %all-to-all-done.1, bf16[16384,256]{1,0:T(8,128)(2,1)} %fusion, bf16[128,256]{1,0:T(8,128)(2,1)S(1)} %copy-done.13, ...), kind=kOutput, calls=%fused_computation.18 | convolution fusion | flops 1098907648 | bytes 42008576 | tf_op jit(solution)/shard_map/dot_general | solution.py:78
  198.9 55.1 %all_to_all.41 = bf16[16,32,32,128]{3,2,1,0:T(8,128)(2,1)S(1)} all-to-all(bf16[16,32,32,128]{3,2,1,0:T(8,128)(2,1)} %bitcast.117), channel_id=1, replica_groups=mesh['dp'=8,'ctx'=16] {'ctx'}, dimensions={0} | all-to-all | bytes 8388608 | tf_op jit(solution)/shard_map/all_to_all | solution.py:15
  256.0 6.3 %convert_bitcast_fusion = bf16[512,32,128]{0,2,1:T(8,128)(2,1)} fusion(bf16[512,32,128]{2,1,0:T(8,128)(2,1)S(1)} %bitcast.135, bf16[512,512]{1,0:T(8,128)(2,1)S(1)} %copy-done), kind=kOutput, calls=%fused_computation.34 | convolution fusion | flops 2149580800 | bytes 8912896 | tf_op jit(solution)/shard_map/mkc,im->ikc/dot_general | solution.py:83
  262.4 7.9 %copy.57 = bf16[512,32,128]{2,1,0:T(8,128)(2,1)} copy(bf16[512,32,128]{0,2,1:T(8,128)(2,1)} %convert_bitcast_fusion) | data formatting | bytes 8388608 | tf_op jit(solution)/shard_map/convert_element_type | solution.py:83
  286.9 6.9 %fusion.31 = f32[512,512]{1,0:T(8,128)} fusion(bf16[512,32,128]{2,1,0:T(8,128)(2,1)} %bitcast.136, bf16[512,32,128]{2,1,0:T(8,128)(2,1)} %bitcast.121), kind=kOutput, calls=%fused_computation.44 | convolution fusion | flops 2147483648 | bytes 9437184 | tf_op jit(solution)/shard_map/ikc,mkc->im/dot_general | solution.py:84
  295.1 32.0 %all-to-all-done.3 = bf16[16,32,32,128]{3,2,1,0:T(8,128)(2,1)} async-done(((bf16[16,32,32,128]{3,2,1,0:T(8,128)(2,1)}), bf16[16,32,32,128]{3,2,1,0:T(8,128)(2,1)}, u32[]{:S(2)}, u32[]{:S(2)}) %all-to-all-start.3) | async-done | bytes 4194336 | tf_op jit(solution)/shard_map/all_to_all | solution.py:15
  327.1 6.6 %fusion.16 = bf16[32,512,128]{1,2,0:T(8,128)(2,1)} fusion(bf16[16,32,32,128]{3,2,1,0:T(8,128)(2,1)} %all-to-all-done.3, bf16[512,16,32,1]{0,2,3,1:T(8,128)(2,1)S(1)} %bitcast.139), kind=kOutput, calls=%fused_computation.30 | convolution fusion | flops 2149580800 | bytes 8912896 | tf_op jit(solution)/shard_map/dirc,jdr->ijc/dot_general | solution.py:88
  333.6 6.5 %copy.59 = bf16[32,512,128]{2,1,0:T(8,128)(2,1)} copy(bf16[32,512,128]{1,2,0:T(8,128)(2,1)} %fusion.16) | data formatting | bytes 8388608 | tf_op jit(solution)/shard_map/dirc,jdr->ijc/transpose | solution.py:88
  340.1 7.0 %fusion.36 = f32[128,256]{0,1:T(8,128)S(1)} fusion(bf16[1,16384,128]{2,1,0:T(8,128)(2,1)} %param.7, bf16[16384,128]{1,0:T(8,128)(2,1)} %bitcast.132, bf16[16384,128]{1,0:T(8,128)(2,1)} %bitcast.128), kind=kOutput, calls=%fused_computation.48 | convolution fusion | flops 1090519040 | bytes 12713984 | tf_op jit(solution)/shard_map/dot_general | solution.py:102
  363.9 6.5 %convolution_dynamic-update-slice_fusion = f32[4864,128]{1,0:T(8,128)} fusion(f32[4864,128]{1,0:T(8,128)} %constant_dynamic-update-slice_fusion, bf16[16384,256]{1,0:T(8,128)(2,1)} %get-tuple-element.14, bf16[16384,128]{1,0:T(8,128)(2,1)S(1)} %bitcast.113), kind=kOutput, calls=%fused_computation.47 | convolution fusion | flops 1073741824 | bytes 12713984 | tf_op jit(solution)/shard_map/dot_general | solution.py:75
  370.4 36.8 %all_to_all.42 = f32[16,304,128]{2,1,0:T(8,128)S(1)} all-to-all(f32[16,304,128]{2,1,0:T(8,128)} %bitcast.137), channel_id=1, replica_groups=mesh['dp'=8,'ctx'=16] {'ctx'}, dimensions={0} | all-to-all | bytes 4980736 | tf_op jit(solution)/shard_map/all_to_all | solution.py:15
  407.4 10.6 %all_to_all.43 = f32[8,38,128]{2,1,0:T(8,128)S(1)} all-to-all(f32[8,38,128]{2,1,0:T(8,128)S(1)} %reshape.105), channel_id=1, replica_groups=mesh['dp'=8,'ctx'=16] {'dp'}, dimensions={0} | all-to-all | bytes 311296 | tf_op jit(solution)/shard_map/all_to_all | solution.py:15
  418.0 8.1 %all_to_all.44 = f32[8,38,128]{2,1,0:T(8,128)S(1)} all-to-all(f32[8,38,128]{2,1,0:T(8,128)S(1)} %broadcast_in_dim.17), channel_id=1, replica_groups=mesh['dp'=8,'ctx'=16] {'dp'}, dimensions={0} | all-to-all | bytes 311296 | tf_op jit(solution)/shard_map/all_to_all | solution.py:15
  427.7 7.4 %all-to-all-start.7 = ((f32[16,304,128]{2,1,0:T(8,128)}), f32[16,304,128]{2,1,0:T(8,128)S(1)}, u32[]{:S(2)}, u32[]{:S(2)}) async-start(f32[16,304,128]{2,1,0:T(8,128)} %broadcast_in_dim.19), calls=%async_computation.7 | async-start | bytes 4980736 | tf_op jit(solution)/shard_map/all_to_all | solution.py:15
  448.7 6.6 %fusion.5 = bf16[1,16384,128]{2,1,0:T(8,128)(2,1)} fusion(f32[16384,128]{1,0:T(8,128)S(1)} %bitcast.126, bf16[128,256]{1,0:T(8,128)(2,1)S(1)} %copy-done.15, bf16[16384,128]{1,0:T(8,128)(2,1)} %bitcast.133, bf16[16384,128]{1,0:T(8,128)(2,1)S(1)} %bitcast.129), kind=kOutput, calls=%fused_computation.9 | convolution fusion | flops 1094713344 | bytes 21037056 | tf_op jit(solution)/shard_map/dot_general | solution.py:104
  455.3 12.5 %all-to-all-done.7 = f32[16,304,128]{2,1,0:T(8,128)S(1)} async-done(((f32[16,304,128]{2,1,0:T(8,128)}), f32[16,304,128]{2,1,0:T(8,128)S(1)}, u32[]{:S(2)}, u32[]{:S(2)}) %all-to-all-start.7) | async-done | bytes 2490400 | tf_op jit(solution)/shard_map/all_to_all | solution.py:15
  (76 shorter events, 93.4 us)
Async XLA Ops:
  0.6 79.1 %copy-start = (bf16[512,512]{1,0:T(8,128)(2,1)S(1)}, bf16[512,512]{1,0:T(8,128)(2,1)}, u32[]{:S(2)}) copy-start(bf16[512,512]{1,0:T(8,128)(2,1)} %param.11) | copy-start | bytes 1572868
  5.2 5.7 %copy-start.1 = (f32[16384,256]{1,0:T(8,128)}, f32[16384,256]{1,0:T(8,128)S(1)}, u32[]{:S(2)}) copy-start(f32[16384,256]{1,0:T(8,128)S(1)} %fusion.18) | copy-start | bytes 50331652
  10.9 2.3 copy-start.12
  77.8 2.0 copy-start.8
  93.7 57.0 %all-to-all-start.1 = ((bf16[16,32,32,128]{3,2,1,0:T(8,128)(2,1)}), bf16[16,32,32,128]{3,2,1,0:T(8,128)(2,1)}, u32[]{:S(2)}, u32[]{:S(2)}) async-start(bf16[16,32,32,128]{3,2,1,0:T(8,128)(2,1)} %bitcast.123), calls=%async_computation.1 | async-start | bytes 8388608 | tf_op jit(solution)/shard_map/all_to_all | solution.py:15
  104.5 4.3 copy-start.7
  108.8 4.4 copy-start.9
  116.3 42.1 %copy-start.13 = (bf16[128,256]{1,0:T(8,128)(2,1)S(1)}, bf16[128,256]{1,0:T(8,128)(2,1)}, u32[]{:S(2)}) copy-start(bf16[128,256]{1,0:T(8,128)(2,1)} %param.12) | copy-start | bytes 196612
  158.4 12.2 %copy-start.4 = (bf16[16384,128]{1,0:T(8,128)(2,1)}, bf16[16384,128]{1,0:T(8,128)(2,1)S(1)}, u32[]{:S(2)}) copy-start(bf16[16384,128]{1,0:T(8,128)(2,1)S(1)} %fusion.7) | copy-start | bytes 12582916
  158.4 12.2 %copy-start.2 = (bf16[32,16,32,128]{3,2,0,1:T(8,128)(2,1)S(1)}, bf16[32,16,32,128]{3,2,0,1:T(8,128)(2,1)}, u32[]{:S(2)}) copy-start(bf16[32,16,32,128]{3,2,0,1:T(8,128)(2,1)} %copy.53) | copy-start | bytes 12582916
  158.4 12.2 %copy-start.14 = (bf16[256,128]{1,0:T(8,128)(2,1)S(1)}, bf16[256,128]{1,0:T(8,128)(2,1)}, u32[]{:S(2)}) copy-start(bf16[256,128]{1,0:T(8,128)(2,1)} %param.13) | copy-start | bytes 196612
  158.4 25.5 %slice-start = ((s8[8388608]{0:T(1024)(128)(4,1)}), s8[4194304]{0:T(1024)(128)(4,1)S(1)}, s32[]{:S(2)}) async-start(s8[8388608]{0:T(1024)(128)(4,1)} %bitcast.109), calls=%async_computation.8 | async-start | bytes 8388608
  170.6 13.3 %slice-start.1 = ((s8[8388608]{0:T(1024)(128)(4,1)}), s8[4194304]{0:T(1024)(128)(4,1)S(1)}, s32[]{:S(2)}) async-start(s8[8388608]{0:T(1024)(128)(4,1)} %bitcast.109), calls=%async_computation.9 | async-start | bytes 8388608
  254.0 2.0 copy-start.11
  270.3 56.7 %all-to-all-start.3 = ((bf16[16,32,32,128]{3,2,1,0:T(8,128)(2,1)}), bf16[16,32,32,128]{3,2,1,0:T(8,128)(2,1)}, u32[]{:S(2)}, u32[]{:S(2)}) async-start(bf16[16,32,32,128]{3,2,1,0:T(8,128)(2,1)} %bitcast.122), calls=%async_computation.3 | async-start | bytes 8388608 | tf_op jit(solution)/shard_map/all_to_all | solution.py:15
  276.2 5.6 %copy-start.5 = (bf16[16384,128]{1,0:T(8,128)(2,1)S(1)}, bf16[16384,128]{1,0:T(8,128)(2,1)}, u32[]{:S(2)}) copy-start(bf16[16384,128]{1,0:T(8,128)(2,1)} %copy-done.4) | copy-start | bytes 12582916
  360.9 2.9 copy-start.3
  427.7 40.1 %all-to-all-start.7 = ((f32[16,304,128]{2,1,0:T(8,128)}), f32[16,304,128]{2,1,0:T(8,128)S(1)}, u32[]{:S(2)}, u32[]{:S(2)}) async-start(f32[16,304,128]{2,1,0:T(8,128)} %broadcast_in_dim.19), calls=%async_computation.7 | async-start | bytes 4980736 | tf_op jit(solution)/shard_map/all_to_all | solution.py:15
  435.1 4.6 copy-start.6
  445.5 3.2 copy-start.10
  445.5 3.2 copy-start.15

commit v2 on v1

--- a/solution.py
+++ b/solution.py
@@ -61,12 +61,12 @@
         wf_q = wf[:, :, q, :]
         first_q = jnp.einsum("ijc,jdr->dirc", value_blocks, wf_q, preferred_element_type=f32).astype(bf16)
         first_mid = a2a(first_q, "ctx").reshape(all_blocks, r_n, width)
-        mixed_mid = jnp.einsum("ikc,im->mkc", first_mid, w_second, preferred_element_type=f32).astype(bf16)
+        mixed_mid = jnp.einsum("im,ikc->mkc", w_second, first_mid, preferred_element_type=f32).astype(bf16)
         mixed = a2a(mixed_mid.reshape(n_ctx, local_blocks, r_n, width), "ctx")
-        mixed = mixed.reshape(-1, width)
-        xq = x5[:, :, q].transpose(1, 0, 2, 3).reshape(-1, width)
-        cq = c5[:, :, q].transpose(1, 0, 2, 3).reshape(-1, width)
-        gq = g5[:, :, q].transpose(1, 0, 2, 3).reshape(-1, width)
+        mixed = mixed.transpose(1, 0, 2, 3).reshape(-1, width)
+        xq = x5[:, :, q].reshape(-1, width)
+        cq = c5[:, :, q].reshape(-1, width)
+        gq = g5[:, :, q].reshape(-1, width)
         mixed32 = mixed.astype(f32)
         hidden = (xq.astype(f32) + gq * mixed32).astype(bf16)
         pre = jnp.dot(hidden, w_up, preferred_element_type=f32)
@@ -78,21 +78,23 @@
         d_hidden = (cq.astype(f32) + jnp.dot(d_act, w_up.T, preferred_element_type=f32)).astype(bf16)
         d_mixed = (d_hidden.astype(f32) * gq).astype(bf16)
         d_gate = d_hidden.astype(f32) * mixed32 * gq * (1.0 - gq)
-        d_mixed_mid = a2a(d_mixed.reshape(n_ctx, local_blocks, r_n, width), "ctx")
+        d_mixed_mid = a2a(d_mixed.reshape(local_blocks, n_ctx, r_n, width).transpose(1, 0, 2, 3), "ctx")
         d_mixed_mid = d_mixed_mid.reshape(all_blocks, r_n, width)
-        d_first_mid = jnp.einsum("mkc,im->ikc", d_mixed_mid, w_second, preferred_element_type=f32).astype(bf16)
+        d_first_mid = jnp.einsum("im,mkc->ikc", w_second, d_mixed_mid, preferred_element_type=f32).astype(bf16)
         grad_second = grad_second + jnp.einsum(
             "ikc,mkc->im", first_mid, d_mixed_mid, preferred_element_type=f32
         )
         d_first = a2a(d_first_mid.reshape(n_ctx, local_blocks, r_n, width), "ctx")
         d_values = d_values + jnp.einsum("dirc,jdr->ijc", d_first, wf_q, preferred_element_type=f32)
         gf_parts.append(jnp.einsum("ijc,dirc->jdr", value_blocks, d_first, preferred_element_type=f32))
-        outs.append(out_q.reshape(n_ctx, local_blocks, r_n, width))
-        d_hiddens.append(d_hidden.reshape(n_ctx, local_blocks, r_n, width))
-        d_gates.append(d_gate.reshape(n_ctx, local_blocks, r_n, width))
+        outs.append(out_q.reshape(local_blocks, n_ctx, r_n, width))
+        d_hiddens.append(d_hidden.reshape(local_blocks, n_ctx, r_n, width))
+        d_gates.append(d_gate.reshape(local_blocks, n_ctx, r_n, width))
 
     def rows_of(parts):
-        return jnp.stack(parts, axis=2).transpose(1, 0, 2, 3, 4).reshape(seq_rows, width)
+        if len(parts) == 1:
+            return parts[0].reshape(seq_rows, width)
+        return jnp.stack(parts, axis=2).reshape(seq_rows, width)
 
     output = rows_of(outs)
     d_hidden = rows_of(d_hiddens)

time: 481 us -> 492 us (1.023)
  blocking collectives: 169 us -> 224 us
  waiting for transfers between devices: 79 us -> 56.1 us
  local copies, waits for them, and re-layouts: 79.1 us -> 63.6 us
    all_to_all x5 -> x6, blocking collectives: 169 us -> 224 us  [a2a(): return lax.all_to_all(x, axis, 0, 0, tiled=True)]
    all_to_all x3 -> x2, waiting for transfers between devices: 79 us -> 56.1 us  [a2a(): return lax.all_to_all(x, axis, 0, 0, tiled=True)]
    another operation x2 -> x0, local copies, waits for them, and re-layouts: 8.63 us -> none  [the longest x1 5.59 us: rows_of(): jnp.stack(parts, axis=2).transpose(1, 0, 2, 3, 4).reshape(seq_rows, width)]
    transpose x2 -> x0, local copies, waits for them, and re-layouts: 7.46 us -> none  [the longest x1 4.31 us: body(): gq = g5[:, :, q].transpose(1, 0, 2, 3).reshape(-1, width)]
    convert_element_type x0 -> x1, other arithmetic: none -> 5.4 us  [body(): mixed32 = mixed.astype(f32)]
    all_to_all x3 -> x2, starting transfers between devices: 19.4 us -> 21.3 us  [a2a(): return lax.all_to_all(x, axis, 0, 0, tiled=True)]
    unnamed x41 -> x45, local copies, waits for them, and re-layouts: 13.5 us -> 14.7 us
    convert_element_type x4 -> x3, local copies, waits for them, and re-layouts: 24.9 us -> 24 us  [the longest x1 8.24 us: body(): mixed32 = mixed.astype(f32)]
  transfers between devices with their start and end apart: 3 -> 2, of which waited for: 3 -> 2; matrix products, arithmetic and copies ran while one was open for 12% -> 6% of each run, Pallas kernels for 0% -> 0%
where the time goes in v2:
time: 492 us; the launch traced here: 487 us
  blocking collectives  224 us (46%)
  matrix products  110 us (22%)
  local copies, waits for them, and re-layouts  63.6 us (13%)
  waiting for transfers between devices  56.1 us (11%)
  starting transfers between devices  21.3 us (4%)
  other arithmetic  10.5 us (2%)
    all_to_all x6, blocking collectives, a2a(): return lax.all_to_all(x, axis, 0, 0, tiled=True)  224 us
    all_to_all x2, waiting for transfers between devices, a2a(): return lax.all_to_all(x, axis, 0, 0, tiled=True)  56.1 us
    all_to_all x2, starting transfers between devices, a2a(): return lax.all_to_all(x, axis, 0, 0, tiled=True)  21.3 us
    unnamed x45, local copies, waits for them, and re-layouts  14.7 us
    dot_general x1, matrix products, body(): jnp.dot(cq, w_down.T, preferred_element_type=f32) * silu_slope(pre)  13.2 us
    dot_general x1, matrix products, body(): jnp.dot(d_act, w_up.T, preferred_element_type=f32)  12.6 us
    dot_general x1, matrix products, body(): pre = jnp.dot(hidden, w_up, preferred_element_type=f32)  12.1 us
  transfers between devices with their start and end apart: 2, of which 2 were waited for; matrix products, arithmetic and copies ran while one was open for 6% of the time, Pallas kernels for 0%

profile of v2, /device:TPU:1, one launch (start us, length us, event | category | flops | bytes accessed | tf_op | source)
XLA Modules:
  0.0 487.4 jit_solution(5181078997631622831)
XLA Ops:
  16.3 58.7 %all_to_all.40 = bf16[16,32,32,128]{3,2,1,0:T(8,128)(2,1)S(1)} all-to-all(bf16[16,32,32,128]{3,2,1,0:T(8,128)(2,1)S(1)} %copy.39), channel_id=1, replica_groups=mesh['dp'=8,'ctx'=16] {'ctx'}, dimensions={0} | all-to-all | bytes 8388608 | tf_op jit(solution)/shard_map/all_to_all | solution.py:15
  83.0 7.8 %copy.41 = bf16[512,32,128]{2,1,0:T(8,128)(2,1)} copy(bf16[512,32,128]{0,2,1:T(8,128)(2,1)} %convert_bitcast_fusion.2) | data formatting | bytes 8388608 | tf_op jit(solution)/shard_map/convert_element_type | solution.py:64
  90.9 55.9 %all_to_all.41 = bf16[16,32,32,128]{3,2,1,0:T(8,128)(2,1)S(1)} all-to-all(bf16[16,32,32,128]{3,2,1,0:T(8,128)(2,1)} %bitcast.105), channel_id=1, replica_groups=mesh['dp'=8,'ctx'=16] {'ctx'}, dimensions={0} | all-to-all | bytes 8388608 | tf_op jit(solution)/shard_map/all_to_all | solution.py:15
  152.2 8.2 %copy.42 = f32[32,16,32,128]{3,2,1,0:T(8,128)} copy(f32[32,16,32,128]{3,2,0,1:T(8,128)} %convert_bitcast_fusion) | data formatting | bytes 16777216 | tf_op jit(solution)/shard_map/convert_element_type | solution.py:70
  165.2 12.1 %multiply_convert_fusion = (bf16[16384,256]{1,0:T(8,128)(2,1)}, f32[16384,256]{1,0:T(8,128)}) fusion(bf16[16384,128]{1,0:T(8,128)(2,1)S(1)} %fusion.11, bf16[128,256]{1,0:T(8,128)(2,1)S(1)} %copy-done.12), kind=kOutput, calls=%fused_computation.11 | convolution fusion | flops 1094713344 | bytes 29425664 | tf_op jit(solution)/shard_map/dot_general | solution.py:72
  177.4 13.2 %fusion = bf16[16384,256]{1,0:T(8,128)(2,1)} fusion(bf16[256,128]{1,0:T(8,128)(2,1)S(1)} %copy-done.10, f32[16384,256]{1,0:T(8,128)} %get-tuple-element.15, bf16[1,16384,128]{2,1,0:T(8,128)(2,1)S(1)} %copy-done.5), kind=kOutput, calls=%fused_computation.1 | convolution fusion | flops 1111490560 | bytes 29425664 | tf_op jit(solution)/shard_map/dot_general | solution.py:76
  190.6 12.6 %fusion.14 = (bf16[16384,128]{1,0:T(8,128)(2,1)}, bf16[16384,128]{1,0:T(8,128)(2,1)}, f32[16384,128]{1,0:T(8,128)}) fusion(f32[32,16,32,128]{3,2,1,0:T(8,128)S(1)} %bitcast.101, f32[16384,256]{1,0:T(8,128)} %copy-done.1, bf16[16384,256]{1,0:T(8,128)(2,1)} %fusion, bf16[128,256]{1,0:T(8,128)(2,1)S(1)} %copy-done.12, bf16[1,16384,128]{2,1,0:T(8,128)(2,1)} %param.8), kind=kOutput, calls=%fused_computation.26 | convolution fusion | flops 1103101952 | bytes 46202880 | tf_op jit(solution)/shard_map/dot_general | solution.py:78
  206.4 54.3 %all_to_all.42 = bf16[16,32,32,128]{3,2,1,0:T(8,128)(2,1)S(1)} all-to-all(bf16[16,32,32,128]{3,2,1,0:T(8,128)(2,1)S(1)} %bitcast.106), channel_id=1, replica_groups=mesh['dp'=8,'ctx'=16] {'ctx'}, dimensions={0} | all-to-all | bytes 8388608 | tf_op jit(solution)/shard_map/all_to_all | solution.py:15
  262.8 6.4 %convert_bitcast_fusion.1 = bf16[512,32,128]{0,2,1:T(8,128)(2,1)} fusion(bf16[512,32,128]{2,1,0:T(8,128)(2,1)S(1)} %bitcast.113, bf16[512,512]{1,0:T(8,128)(2,1)S(1)} %copy-done), kind=kOutput, calls=%fused_computation.38 | convolution fusion | flops 2149580800 | bytes 8912896 | tf_op jit(solution)/shard_map/im,mkc->ikc/dot_general | solution.py:83
  269.1 7.9 %copy.45 = bf16[512,32,128]{2,1,0:T(8,128)(2,1)} copy(bf16[512,32,128]{0,2,1:T(8,128)(2,1)} %convert_bitcast_fusion.1) | data formatting | bytes 8388608 | tf_op jit(solution)/shard_map/convert_element_type | solution.py:83
  277.1 13.8 %all-to-all-start.3 = ((bf16[16,32,32,128]{3,2,1,0:T(8,128)(2,1)}), bf16[16,32,32,128]{3,2,1,0:T(8,128)(2,1)}, u32[]{:S(2)}, u32[]{:S(2)}) async-start(bf16[16,32,32,128]{3,2,1,0:T(8,128)(2,1)} %bitcast.104), calls=%async_computation.3 | async-start | bytes 8388608 | tf_op jit(solution)/shard_map/all_to_all | solution.py:15
  290.9 6.2 %fusion.51 = f32[128,256]{1,0:T(8,128)S(1)} fusion(bf16[16384,128]{1,0:T(8,128)(2,1)} %copy-done.2, bf16[16384,256]{1,0:T(8,128)(2,1)} %fusion), kind=kOutput, calls=%fused_computation.63 | convolution fusion | flops 1073741824 | bytes 12713984 | tf_op jit(solution)/shard_map/dot_general | solution.py:77
  303.1 38.7 %all-to-all-done.3 = bf16[16,32,32,128]{3,2,1,0:T(8,128)(2,1)} async-done(((bf16[16,32,32,128]{3,2,1,0:T(8,128)(2,1)}), bf16[16,32,32,128]{3,2,1,0:T(8,128)(2,1)}, u32[]{:S(2)}, u32[]{:S(2)}) %all-to-all-start.3) | async-done | bytes 4194336 | tf_op jit(solution)/shard_map/all_to_all | solution.py:15
  341.8 6.6 %fusion.16 = bf16[32,512,128]{1,2,0:T(8,128)(2,1)} fusion(bf16[16,32,32,128]{3,2,1,0:T(8,128)(2,1)} %all-to-all-done.3, bf16[512,16,32,1]{0,2,3,1:T(8,128)(2,1)S(1)} %bitcast.118), kind=kOutput, calls=%fused_computation.30 | convolution fusion | flops 2149580800 | bytes 8912896 | tf_op jit(solution)/shard_map/dirc,jdr->ijc/dot_general | solution.py:88
  348.4 6.5 %copy.47 = bf16[32,512,128]{2,1,0:T(8,128)(2,1)} copy(bf16[32,512,128]{1,2,0:T(8,128)(2,1)} %fusion.16) | data formatting | bytes 8388608 | tf_op jit(solution)/shard_map/dirc,jdr->ijc/transpose | solution.py:88
  354.8 7.0 %fusion.42 = f32[128,256]{0,1:T(8,128)S(1)} fusion(bf16[1,16384,128]{2,1,0:T(8,128)(2,1)} %param.7, bf16[16384,128]{1,0:T(8,128)(2,1)} %bitcast.111, bf16[16384,128]{1,0:T(8,128)(2,1)} %get-tuple-element.7), kind=kOutput, calls=%fused_computation.52 | convolution fusion | flops 1090519040 | bytes 12713984 | tf_op jit(solution)/shard_map/dot_general | solution.py:104
  378.6 6.5 %fusion.39 = f32[4864,128]{1,0:T(8,128)} fusion(f32[4864,128]{1,0:T(8,128)} %constant_dynamic-update-slice_fusion, bf16[16384,256]{1,0:T(8,128)(2,1)} %get-tuple-element.14, bf16[1,16384,128]{2,1,0:T(8,128)(2,1)S(1)} %copy-done.6), kind=kOutput, calls=%fused_computation.51 | convolution fusion | flops 1073741824 | bytes 12713984 | tf_op jit(solution)/shard_map/dot_general | solution.py:75
  385.2 36.9 %all_to_all.43 = f32[16,304,128]{2,1,0:T(8,128)S(1)} all-to-all(f32[16,304,128]{2,1,0:T(8,128)} %bitcast.116), channel_id=1, replica_groups=mesh['dp'=8,'ctx'=16] {'ctx'}, dimensions={0} | all-to-all | bytes 4980736 | tf_op jit(solution)/shard_map/all_to_all | solution.py:15
  422.2 10.5 %all_to_all.44 = f32[8,38,128]{2,1,0:T(8,128)S(1)} all-to-all(f32[8,38,128]{2,1,0:T(8,128)S(1)} %reshape.82), channel_id=1, replica_groups=mesh['dp'=8,'ctx'=16] {'dp'}, dimensions={0} | all-to-all | bytes 311296 | tf_op jit(solution)/shard_map/all_to_all | solution.py:15
  432.7 8.1 %all_to_all.45 = f32[8,38,128]{2,1,0:T(8,128)S(1)} all-to-all(f32[8,38,128]{2,1,0:T(8,128)S(1)} %broadcast_in_dim.17), channel_id=1, replica_groups=mesh['dp'=8,'ctx'=16] {'dp'}, dimensions={0} | all-to-all | bytes 311296 | tf_op jit(solution)/shard_map/all_to_all | solution.py:15
  442.4 7.4 %all-to-all-start.7 = ((f32[16,304,128]{2,1,0:T(8,128)}), f32[16,304,128]{2,1,0:T(8,128)S(1)}, u32[]{:S(2)}, u32[]{:S(2)}) async-start(f32[16,304,128]{2,1,0:T(8,128)} %broadcast_in_dim.19), calls=%async_computation.7 | async-start | bytes 4980736 | tf_op jit(solution)/shard_map/all_to_all | solution.py:15
  449.9 9.1 %fusion.6 = bf16[1,16384,128]{2,1,0:T(8,128)(2,1)} fusion(bf16[16384,256]{1,0:T(8,128)(2,1)} %get-tuple-element.14, bf16[256,128]{1,0:T(8,128)(2,1)S(1)} %copy-done.10, bf16[16384,128]{1,0:T(8,128)(2,1)} %copy-done.2), kind=kOutput, calls=%fused_computation.10 | convolution fusion | flops 1080033280 | bytes 16842752 | tf_op jit(solution)/shard_map/dot_general | solution.py:74
  459.0 6.1 %fusion.5 = bf16[1,16384,128]{2,1,0:T(8,128)(2,1)} fusion(f32[16384,128]{1,0:T(8,128)} %get-tuple-element.16, bf16[128,256]{1,0:T(8,128)(2,1)S(1)} %copy-done.11, bf16[16384,128]{1,0:T(8,128)(2,1)S(1)} %bitcast.112, bf16[16384,128]{1,0:T(8,128)(2,1)S(1)} %copy-done.13), kind=kOutput, calls=%fused_computation.9 | convolution fusion | flops 1094713344 | bytes 21037056 | tf_op jit(solution)/shard_map/dot_general | solution.py:106
  465.1 17.5 %all-to-all-done.7 = f32[16,304,128]{2,1,0:T(8,128)S(1)} async-done(((f32[16,304,128]{2,1,0:T(8,128)}), f32[16,304,128]{2,1,0:T(8,128)S(1)}, u32[]{:S(2)}, u32[]{:S(2)}) %all-to-all-start.7) | async-done | bytes 2490400 | tf_op jit(solution)/shard_map/all_to_all | solution.py:15
  (76 shorter events, 68.2 us)
Async XLA Ops:
  0.6 76.3 %copy-start = (bf16[512,512]{1,0:T(8,128)(2,1)S(1)}, bf16[512,512]{1,0:T(8,128)(2,1)}, u32[]{:S(2)}) copy-start(bf16[512,512]{1,0:T(8,128)(2,1)} %param.11) | copy-start | bytes 1572868
  6.5 5.7 %copy-start.1 = (f32[16384,256]{1,0:T(8,128)}, f32[16384,256]{1,0:T(8,128)S(1)}, u32[]{:S(2)}) copy-start(f32[16384,256]{1,0:T(8,128)S(1)} %fusion.21) | copy-start | bytes 50331652
  12.8 2.4 copy-start.7
  75.0 2.0 copy-start.4
  90.9 69.6 %slice-start = ((s8[16777216]{0:T(1024)(128)(4,1)}), s8[4194304]{0:T(1024)(128)(4,1)S(1)}, s32[]{:S(2)}) async-start(s8[16777216]{0:T(1024)(128)(4,1)} %bitcast.98), calls=%async_computation.8 | async-start | bytes 8388608
  146.8 13.7 %slice-start.1 = ((s8[16777216]{0:T(1024)(128)(4,1)}), s8[4194304]{0:T(1024)(128)(4,1)S(1)}, s32[]{:S(2)}) async-start(s8[16777216]{0:T(1024)(128)(4,1)} %bitcast.98), calls=%async_computation.9 | async-start | bytes 8388608
  146.8 13.7 %slice-start.2 = ((s8[16777216]{0:T(1024)(128)(4,1)}), s8[4194304]{0:T(1024)(128)(4,1)S(1)}, s32[]{:S(2)}) async-start(s8[16777216]{0:T(1024)(128)(4,1)} %bitcast.98), calls=%async_computation.10 | async-start | bytes 8388608
  152.2 8.3 %slice-start.3 = ((s8[16777216]{0:T(1024)(128)(4,1)}), s8[4194304]{0:T(1024)(128)(4,1)S(1)}, s32[]{:S(2)}) async-start(s8[16777216]{0:T(1024)(128)(4,1)} %bitcast.98), calls=%async_computation.11 | async-start | bytes 8388608
  152.2 8.3 %copy-start.3 = (bf16[1,16384,128]{2,1,0:T(8,128)(2,1)S(1)}, bf16[1,16384,128]{2,1,0:T(8,128)(2,1)}, u32[]{:S(2)}) copy-start(bf16[1,16384,128]{2,1,0:T(8,128)(2,1)} %param.7) | copy-start | bytes 12582916
  160.5 4.7 copy-start.12
  165.2 12.2 %copy-start.2 = (bf16[16384,128]{1,0:T(8,128)(2,1)}, bf16[16384,128]{1,0:T(8,128)(2,1)S(1)}, u32[]{:S(2)}) copy-start(bf16[16384,128]{1,0:T(8,128)(2,1)S(1)} %fusion.11) | copy-start | bytes 12582916
  165.2 12.2 %copy-start.5 = (bf16[1,16384,128]{2,1,0:T(8,128)(2,1)S(1)}, bf16[1,16384,128]{2,1,0:T(8,128)(2,1)}, u32[]{:S(2)}) copy-start(bf16[1,16384,128]{2,1,0:T(8,128)(2,1)} %param.8) | copy-start | bytes 12582916
  165.2 12.2 %copy-start.10 = (bf16[256,128]{1,0:T(8,128)(2,1)S(1)}, bf16[256,128]{1,0:T(8,128)(2,1)}, u32[]{:S(2)}) copy-start(bf16[256,128]{1,0:T(8,128)(2,1)} %param.13) | copy-start | bytes 196612
  165.2 25.3 %slice-start.4 = ((s8[8388608]{0:T(1024)(128)(4,1)}), s8[4194304]{0:T(1024)(128)(4,1)S(1)}, s32[]{:S(2)}) async-start(s8[8388608]{0:T(1024)(128)(4,1)} %bitcast.100), calls=%async_computation.12 | async-start | bytes 8388608
  177.4 13.2 %slice-start.5 = ((s8[8388608]{0:T(1024)(128)(4,1)}), s8[4194304]{0:T(1024)(128)(4,1)S(1)}, s32[]{:S(2)}) async-start(s8[8388608]{0:T(1024)(128)(4,1)} %bitcast.100), calls=%async_computation.13 | async-start | bytes 8388608
  260.8 2.0 copy-start.9
  277.1 64.7 %all-to-all-start.3 = ((bf16[16,32,32,128]{3,2,1,0:T(8,128)(2,1)}), bf16[16,32,32,128]{3,2,1,0:T(8,128)(2,1)}, u32[]{:S(2)}, u32[]{:S(2)}) async-start(bf16[16,32,32,128]{3,2,1,0:T(8,128)(2,1)} %bitcast.104), calls=%async_computation.3 | async-start | bytes 8388608 | tf_op jit(solution)/shard_map/all_to_all | solution.py:15
  375.7 2.9 copy-start.6
  442.4 40.1 %all-to-all-start.7 = ((f32[16,304,128]{2,1,0:T(8,128)}), f32[16,304,128]{2,1,0:T(8,128)S(1)}, u32[]{:S(2)}, u32[]{:S(2)}) async-start(f32[16,304,128]{2,1,0:T(8,128)} %broadcast_in_dim.19), calls=%async_computation.7 | async-start | bytes 4980736 | tf_op jit(solution)/shard_map/all_to_all | solution.py:15
  449.8 9.1 %copy-start.8 = (bf16[32,512,128]{2,1,0:T(8,128)(2,1)S(1)}, bf16[32,512,128]{2,1,0:T(8,128)(2,1)}, u32[]{:S(2)}) copy-start(bf16[32,512,128]{2,1,0:T(8,128)(2,1)} %copy.47) | copy-start | bytes 12582916
  449.8 9.1 %copy-start.11 = (bf16[128,256]{1,0:T(8,128)(2,1)S(1)}, bf16[128,256]{1,0:T(8,128)(2,1)}, u32[]{:S(2)}) copy-start(bf16[128,256]{1,0:T(8,128)(2,1)} %param.9) | copy-start | bytes 196612
  449.9 9.1 %copy-start.13 = (bf16[16384,128]{1,0:T(8,128)(2,1)S(1)}, bf16[16384,128]{1,0:T(8,128)(2,1)}, u32[]{:S(2)}) copy-start(bf16[16384,128]{1,0:T(8,128)(2,1)} %get-tuple-element.7) | copy-start | bytes 12582916

commit v3 on v1

--- a/solution.py
+++ b/solution.py
@@ -11,21 +11,31 @@
     return sigma * (1.0 + pre * (1.0 - sigma))
 
 
-def a2a(x, axis):
-    return lax.all_to_all(x, axis, 0, 0, tiled=True)
+def a2a(x, axis, groups=None):
+    return lax.all_to_all(x, axis, 0, 0, tiled=True, axis_index_groups=groups)
 
 
 def all_reduce_a2a(flat):
     n_ctx = lax.axis_size("ctx")
     n_dp = lax.axis_size("dp")
     rows, width = flat.shape
-    part = rows // n_ctx
+    core = lax.axis_index("ctx") % 2
+    pairs = [(i, i ^ 1) for i in range(n_ctx)]
+    groups = [list(range(0, n_ctx, 2)), list(range(1, n_ctx, 2))]
+    chips = n_ctx // 2
+    half = rows // 2
+    part = half // chips
     piece = part // n_dp
-    a = a2a(flat.reshape(n_ctx, part, width), "ctx").sum(0)
+    halves = flat.reshape(2, half, width)
+    mine = jnp.where(core == 0, halves[0], halves[1])
+    other = jnp.where(core == 0, halves[1], halves[0])
+    s1 = mine + lax.ppermute(other, "ctx", pairs)
+    a = a2a(s1.reshape(chips, part, width), "ctx", groups).sum(0)
     b = a2a(a.reshape(n_dp, piece, width), "dp").sum(0)
     c = a2a(jnp.broadcast_to(b[None], (n_dp, piece, width)), "dp").reshape(part, width)
-    d = a2a(jnp.broadcast_to(c[None], (n_ctx, part, width)), "ctx").reshape(rows, width)
-    return d
+    d = a2a(jnp.broadcast_to(c[None], (chips, part, width)), "ctx", groups).reshape(half, width)
+    e = lax.ppermute(d, "ctx", pairs)
+    return jnp.where(core == 0, jnp.concatenate([d, e]), jnp.concatenate([e, d]))
 
 
 def body(tokens, cotangent, w_gate_value, w_first, w_second, w_up, w_down):

time: 481 us -> 471 us (0.979)
  blocking collectives: 169 us -> 124 us
  waiting for transfers between devices: 79 us -> 112 us
  local copies, waits for them, and re-layouts: 79.1 us -> 72.6 us
  starting transfers between devices: 19.4 us -> 25.9 us
    all_to_all x5, blocking collectives: 169 us -> 124 us  [a2a(): return lax.all_to_all(x, axis, 0, 0, tiled=True, axis_index_groups=groups)]
    all_to_all x3, waiting for transfers between devices: 79 us -> 109 us  [a2a(): return lax.all_to_all(x, axis, 0, 0, tiled=True, axis_index_groups=groups)]
    ppermute x0 -> x2, starting transfers between devices: none -> 6.21 us  [the longest x1 5.12 us: all_reduce_a2a(): e = lax.ppermute(d, 'ctx', pairs)]
    unnamed x41 -> x33, local copies, waits for them, and re-layouts: 13.5 us -> 9.09 us
  transfers between devices with their start and end apart: 3 -> 5, of which waited for: 3 -> 4; matrix products, arithmetic and copies ran while one was open for 12% -> 14% of each run, Pallas kernels for 0% -> 0%
where the time goes in v3:
time: 471 us; the launch traced here: 462 us
  blocking collectives  124 us (26%)
  matrix products  114 us (24%)
  waiting for transfers between devices  112 us (24%)
  local copies, waits for them, and re-layouts  72.6 us (15%)
  starting transfers between devices  25.9 us (5%)
  other arithmetic  12.9 us (3%)
    all_to_all x5, blocking collectives, a2a(): return lax.all_to_all(x, axis, 0, 0, tiled=True, axis_index_groups=groups)  124 us
    all_to_all x3, waiting for transfers between devices, a2a(): return lax.all_to_all(x, axis, 0, 0, tiled=True, axis_index_groups=groups)  109 us
    all_to_all x3, starting transfers between devices, a2a(): return lax.all_to_all(x, axis, 0, 0, tiled=True, axis_index_groups=groups)  19.7 us
    dot_general x1, matrix products, body(): jnp.dot(d_act, w_up.T, preferred_element_type=f32)  15.3 us
    dot_general x1, matrix products, body(): jnp.dot(cq, w_down.T, preferred_element_type=f32) * silu_slope(pre)  13.2 us
    dot_general x1, matrix products, body(): pre = jnp.dot(hidden, w_up, preferred_element_type=f32)  12.1 us
  transfers between devices with their start and end apart: 5, of which 4 were waited for; matrix products, arithmetic and copies ran while one was open for 14% of the time, Pallas kernels for 0%

profile of v3, /device:TPU:1, one launch (start us, length us, event | category | flops | bytes accessed | tf_op | source)
XLA Modules:
  0.0 462.2 jit_solution(13001691909745448523)
XLA Ops:
  18.3 8.5 %all-to-all-start = ((bf16[16,32,32,128]{3,2,1,0:T(8,128)(2,1)}), bf16[16,32,32,128]{3,2,1,0:T(8,128)(2,1)}, u32[]{:S(2)}, u32[]{:S(2)}) async-start(bf16[16,32,32,128]{3,2,1,0:T(8,128)(2,1)} %copy.49), calls=%async_computation | async-start | bytes 8388608 | tf_op jit(solution)/shard_map/all_to_all | solution.py:15
  36.7 40.9 %all-to-all-done = bf16[16,32,32,128]{3,2,1,0:T(8,128)(2,1)} async-done(((bf16[16,32,32,128]{3,2,1,0:T(8,128)(2,1)}), bf16[16,32,32,128]{3,2,1,0:T(8,128)(2,1)}, u32[]{:S(2)}, u32[]{:S(2)}) %all-to-all-start) | async-done | bytes 4194336 | tf_op jit(solution)/shard_map/all_to_all | solution.py:15
  77.7 7.9 %convert_bitcast_fusion.1 = bf16[512,32,128]{0,2,1:T(8,128)(2,1)} fusion(bf16[512,32,128]{2,1,0:T(8,128)(2,1)} %bitcast.13, bf16[512,512]{1,0:T(8,128)(2,1)S(1)} %copy-done), kind=kOutput, calls=%fused_computation.35 | convolution fusion | flops 2149580800 | bytes 8912896 | tf_op jit(solution)/shard_map/ikc,im->mkc/dot_general | solution.py:74
  85.5 7.8 %copy.51 = bf16[512,32,128]{2,1,0:T(8,128)(2,1)} copy(bf16[512,32,128]{0,2,1:T(8,128)(2,1)} %convert_bitcast_fusion.1) | data formatting | bytes 8388608 | tf_op jit(solution)/shard_map/convert_element_type | solution.py:74
  107.9 42.0 %all-to-all-done.1 = bf16[16,32,32,128]{3,2,1,0:T(8,128)(2,1)} async-done(((bf16[16,32,32,128]{3,2,1,0:T(8,128)(2,1)}), bf16[16,32,32,128]{3,2,1,0:T(8,128)(2,1)}, u32[]{:S(2)}, u32[]{:S(2)}) %all-to-all-start.1) | async-done | bytes 4194336 | tf_op jit(solution)/shard_map/all_to_all | solution.py:15
  149.9 7.6 %fusion.7 = bf16[16384,128]{1,0:T(8,128)(2,1)S(1)} fusion(f32[32,16,32,128]{3,2,0,1:T(8,128)} %copy.46, f32[16,32,32,128]{3,2,1,0:T(8,128)} %copy.47, bf16[16,32,32,128]{3,2,1,0:T(8,128)(2,1)} %all-to-all-done.1), kind=kLoop, calls=%fused_computation.15 | loop fusion | flops 8388608 | bytes 25165824 | tf_op jit(solution)/shard_map/convert_element_type | solution.py:81
  157.6 12.1 %multiply_convert_fusion = (bf16[16384,256]{1,0:T(8,128)(2,1)}, f32[16384,256]{1,0:T(8,128)}) fusion(bf16[16384,128]{1,0:T(8,128)(2,1)S(1)} %fusion.7, bf16[128,256]{1,0:T(8,128)(2,1)S(1)} %copy-done.9), kind=kOutput, calls=%fused_computation.10 | convolution fusion | flops 1094713344 | bytes 29425664 | tf_op jit(solution)/shard_map/dot_general | solution.py:82
  169.8 13.2 %fusion = bf16[16384,256]{1,0:T(8,128)(2,1)} fusion(bf16[16384,128]{1,0:T(8,128)(2,1)S(1)} %bitcast.112, bf16[256,128]{1,0:T(8,128)(2,1)S(1)} %copy-done.10, f32[16384,256]{1,0:T(8,128)} %get-tuple-element.15), kind=kOutput, calls=%fused_computation.1 | convolution fusion | flops 1111490560 | bytes 29425664 | tf_op jit(solution)/shard_map/dot_general | solution.py:86
  182.9 15.3 %fusion.10 = (bf16[16384,128]{1,0:T(8,128)(2,1)}, bf16[16384,128]{1,0:T(8,128)(2,1)}, f32[16384,128]{1,0:T(8,128)}) fusion(f32[16,32,32,128]{3,2,1,0:T(8,128)S(1)} %bitcast.110, bf16[16,32,32,128]{3,2,1,0:T(8,128)(2,1)} %all-to-all-done.1, bf16[16384,256]{1,0:T(8,128)(2,1)} %fusion, bf16[128,256]{1,0:T(8,128)(2,1)S(1)} %copy-done.9, ...), kind=kOutput, calls=%fused_computation.18 | convolution fusion | flops 1098907648 | bytes 42008576 | tf_op jit(solution)/shard_map/dot_general | solution.py:88
  198.2 65.1 %all_to_all.40 = bf16[16,32,32,128]{3,2,1,0:T(8,128)(2,1)S(1)} all-to-all(bf16[16,32,32,128]{3,2,1,0:T(8,128)(2,1)} %bitcast.119), channel_id=1, replica_groups=mesh['dp'=8,'ctx'=16] {'ctx'}, dimensions={0} | all-to-all | bytes 8388608 | tf_op jit(solution)/shard_map/all_to_all | solution.py:15
  265.3 6.3 %convert_bitcast_fusion = bf16[512,32,128]{0,2,1:T(8,128)(2,1)} fusion(bf16[512,32,128]{2,1,0:T(8,128)(2,1)S(1)} %bitcast.135, bf16[512,512]{1,0:T(8,128)(2,1)S(1)} %copy-done), kind=kOutput, calls=%fused_computation.34 | convolution fusion | flops 2149580800 | bytes 8912896 | tf_op jit(solution)/shard_map/mkc,im->ikc/dot_general | solution.py:93
  271.6 8.0 %copy.57 = bf16[512,32,128]{2,1,0:T(8,128)(2,1)} copy(bf16[512,32,128]{0,2,1:T(8,128)(2,1)} %convert_bitcast_fusion) | data formatting | bytes 8388608 | tf_op jit(solution)/shard_map/convert_element_type | solution.py:93
  285.1 6.2 %fusion.47 = f32[128,256]{1,0:T(8,128)S(1)} fusion(bf16[16384,128]{1,0:T(8,128)(2,1)} %copy-done.4, bf16[16384,256]{1,0:T(8,128)(2,1)} %fusion), kind=kOutput, calls=%fused_computation.61 | convolution fusion | flops 1073741824 | bytes 12713984 | tf_op jit(solution)/shard_map/dot_general | solution.py:87
  296.9 6.1 %fusion.48 = f32[256,128]{1,0:T(8,128)S(1)} fusion(bf16[16384,256]{1,0:T(8,128)(2,1)} %get-tuple-element.14, bf16[16384,128]{1,0:T(8,128)(2,1)S(1)} %bitcast.113), kind=kOutput, calls=%fused_computation.62 | convolution fusion | flops 1073741824 | bytes 12713984 | tf_op jit(solution)/shard_map/dot_general | solution.py:85
  309.9 26.2 %all-to-all-done.3 = bf16[16,32,32,128]{3,2,1,0:T(8,128)(2,1)} async-done(((bf16[16,32,32,128]{3,2,1,0:T(8,128)(2,1)}), bf16[16,32,32,128]{3,2,1,0:T(8,128)(2,1)}, u32[]{:S(2)}, u32[]{:S(2)}) %all-to-all-start.3) | async-done | bytes 4194336 | tf_op jit(solution)/shard_map/all_to_all | solution.py:15
  336.1 6.6 %fusion.16 = bf16[32,512,128]{1,2,0:T(8,128)(2,1)} fusion(bf16[16,32,32,128]{3,2,1,0:T(8,128)(2,1)} %all-to-all-done.3, bf16[512,16,32,1]{0,2,3,1:T(8,128)(2,1)S(1)} %bitcast.139), kind=kOutput, calls=%fused_computation.30 | convolution fusion | flops 2149580800 | bytes 8912896 | tf_op jit(solution)/shard_map/dirc,jdr->ijc/dot_general | solution.py:98
  342.7 6.6 %copy.59 = bf16[32,512,128]{2,1,0:T(8,128)(2,1)} copy(bf16[32,512,128]{1,2,0:T(8,128)(2,1)} %fusion.16) | data formatting | bytes 8388608 | tf_op jit(solution)/shard_map/dirc,jdr->ijc/transpose | solution.py:98
  349.3 7.0 %fusion.37 = f32[128,256]{0,1:T(8,128)S(1)} fusion(bf16[1,16384,128]{2,1,0:T(8,128)(2,1)} %param.7, bf16[16384,128]{1,0:T(8,128)(2,1)} %bitcast.133, bf16[16384,128]{1,0:T(8,128)(2,1)} %bitcast.131), kind=kOutput, calls=%fused_computation.53 | convolution fusion | flops 1090519040 | bytes 12713984 | tf_op jit(solution)/shard_map/dot_general | solution.py:112
  373.3 21.3 %all_to_all.41 = f32[8,304,128]{2,1,0:T(8,128)S(1)} all-to-all(f32[8,304,128]{2,1,0:T(8,128)S(1)} %bitcast.127), channel_id=1, replica_groups={{0,2,4,6,8,10,12,14},{1,3,5,7,9,11,13,15},{16,18,20,22,24,26,28,30},{17..., dimensions={0} | all-to-all | bytes 2490368 | tf_op jit(solution)/shard_map/all_to_all | solution.py:15
  394.6 10.5 %all_to_all.42 = f32[8,38,128]{2,1,0:T(8,128)S(1)} all-to-all(f32[8,38,128]{2,1,0:T(8,128)S(1)} %reshape.110), channel_id=1, replica_groups=mesh['dp'=8,'ctx'=16] {'dp'}, dimensions={0} | all-to-all | bytes 311296 | tf_op jit(solution)/shard_map/all_to_all | solution.py:15
  405.2 8.2 %all_to_all.43 = f32[8,38,128]{2,1,0:T(8,128)S(1)} all-to-all(f32[8,38,128]{2,1,0:T(8,128)S(1)} %broadcast_in_dim.17), channel_id=1, replica_groups=mesh['dp'=8,'ctx'=16] {'dp'}, dimensions={0} | all-to-all | bytes 311296 | tf_op jit(solution)/shard_map/all_to_all | solution.py:15
  413.5 18.9 %all_to_all.44 = f32[8,304,128]{2,1,0:T(8,128)S(1)} all-to-all(f32[8,304,128]{2,1,0:T(8,128)S(1)} %broadcast_in_dim.19), channel_id=1, replica_groups={{0,2,4,6,8,10,12,14},{1,3,5,7,9,11,13,15},{16,18,20,22,24,26,28,30},{17..., dimensions={0} | all-to-all | bytes 2490368 | tf_op jit(solution)/shard_map/all_to_all | solution.py:15
  437.5 6.9 %fusion.1 = bf16[16384,128]{1,0:T(8,128)(2,1)S(1)} fusion(bf16[16384,256]{1,0:T(8,128)(2,1)} %get-tuple-element.14, bf16[256,128]{1,0:T(8,128)(2,1)S(1)} %copy-done.10, bf16[16384,128]{1,0:T(8,128)(2,1)} %copy-done.4), kind=kOutput, calls=%fused_computation.5 | convolution fusion | flops 1080033280 | bytes 16842752 | tf_op jit(solution)/shard_map/dot_general | solution.py:84
  449.0 7.9 %fusion.5 = bf16[1,16384,128]{2,1,0:T(8,128)(2,1)} fusion(f32[16384,128]{1,0:T(8,128)S(1)} %bitcast.124, bf16[128,256]{1,0:T(8,128)(2,1)S(1)} %copy-done.11, bf16[16384,128]{1,0:T(8,128)(2,1)} %bitcast.134, bf16[16384,128]{1,0:T(8,128)(2,1)} %bitcast.132), kind=kOutput, calls=%fused_computation.9 | convolution fusion | flops 1094713344 | bytes 21037056 | tf_op jit(solution)/shard_map/dot_general | solution.py:114
  (75 shorter events, 93.7 us)
Async XLA Ops:
  0.6 77.0 %copy-start = (bf16[512,512]{1,0:T(8,128)(2,1)S(1)}, bf16[512,512]{1,0:T(8,128)(2,1)}, u32[]{:S(2)}) copy-start(bf16[512,512]{1,0:T(8,128)(2,1)} %param.11) | copy-start | bytes 1572868
  6.5 5.7 %copy-start.1 = (f32[16384,256]{1,0:T(8,128)}, f32[16384,256]{1,0:T(8,128)S(1)}, u32[]{:S(2)}) copy-start(f32[16384,256]{1,0:T(8,128)S(1)} %fusion.18) | copy-start | bytes 50331652
  12.8 2.4 copy-start.6
  18.3 59.4 %all-to-all-start = ((bf16[16,32,32,128]{3,2,1,0:T(8,128)(2,1)}), bf16[16,32,32,128]{3,2,1,0:T(8,128)(2,1)}, u32[]{:S(2)}, u32[]{:S(2)}) async-start(bf16[16,32,32,128]{3,2,1,0:T(8,128)(2,1)} %copy.49), calls=%async_computation | async-start | bytes 8388608 | tf_op jit(solution)/shard_map/all_to_all | solution.py:15
  26.7 5.5 %copy-start.5 = (bf16[1,16384,128]{2,1,0:T(8,128)(2,1)S(1)}, bf16[1,16384,128]{2,1,0:T(8,128)(2,1)}, u32[]{:S(2)}) copy-start(bf16[1,16384,128]{2,1,0:T(8,128)(2,1)} %param.7) | copy-start | bytes 12582916
  93.4 56.6 %all-to-all-start.1 = ((bf16[16,32,32,128]{3,2,1,0:T(8,128)(2,1)}), bf16[16,32,32,128]{3,2,1,0:T(8,128)(2,1)}, u32[]{:S(2)}, u32[]{:S(2)}) async-start(bf16[16,32,32,128]{3,2,1,0:T(8,128)(2,1)} %bitcast.123), calls=%async_computation.1 | async-start | bytes 8388608 | tf_op jit(solution)/shard_map/all_to_all | solution.py:15
  107.9 49.6 %copy-start.9 = (bf16[128,256]{1,0:T(8,128)(2,1)S(1)}, bf16[128,256]{1,0:T(8,128)(2,1)}, u32[]{:S(2)}) copy-start(bf16[128,256]{1,0:T(8,128)(2,1)} %param.12) | copy-start | bytes 196612
  157.6 12.2 %copy-start.4 = (bf16[16384,128]{1,0:T(8,128)(2,1)}, bf16[16384,128]{1,0:T(8,128)(2,1)S(1)}, u32[]{:S(2)}) copy-start(bf16[16384,128]{1,0:T(8,128)(2,1)S(1)} %fusion.7) | copy-start | bytes 12582916
  157.6 12.2 %copy-start.2 = (bf16[32,16,32,128]{3,2,0,1:T(8,128)(2,1)S(1)}, bf16[32,16,32,128]{3,2,0,1:T(8,128)(2,1)}, u32[]{:S(2)}) copy-start(bf16[32,16,32,128]{3,2,0,1:T(8,128)(2,1)} %copy.53) | copy-start | bytes 12582916
  157.6 12.2 %copy-start.10 = (bf16[256,128]{1,0:T(8,128)(2,1)S(1)}, bf16[256,128]{1,0:T(8,128)(2,1)}, u32[]{:S(2)}) copy-start(bf16[256,128]{1,0:T(8,128)(2,1)} %param.13) | copy-start | bytes 196612
  157.6 25.3 %slice-start = ((s8[8388608]{0:T(1024)(128)(4,1)}), s8[4194304]{0:T(1024)(128)(4,1)S(1)}, s32[]{:S(2)}) async-start(s8[8388608]{0:T(1024)(128)(4,1)} %bitcast.109), calls=%async_computation.8 | async-start | bytes 8388608
  169.7 13.2 %slice-start.1 = ((s8[8388608]{0:T(1024)(128)(4,1)}), s8[4194304]{0:T(1024)(128)(4,1)S(1)}, s32[]{:S(2)}) async-start(s8[8388608]{0:T(1024)(128)(4,1)} %bitcast.109), calls=%async_computation.9 | async-start | bytes 8388608
  263.3 2.0 copy-start.7
  279.6 56.5 %all-to-all-start.3 = ((bf16[16,32,32,128]{3,2,1,0:T(8,128)(2,1)}), bf16[16,32,32,128]{3,2,1,0:T(8,128)(2,1)}, u32[]{:S(2)}, u32[]{:S(2)}) async-start(bf16[16,32,32,128]{3,2,1,0:T(8,128)(2,1)} %bitcast.122), calls=%async_computation.3 | async-start | bytes 8388608 | tf_op jit(solution)/shard_map/all_to_all | solution.py:15
  291.3 5.6 %copy-start.3 = (bf16[32,16,32,128]{3,2,0,1:T(8,128)(2,1)S(1)}, bf16[32,16,32,128]{3,2,0,1:T(8,128)(2,1)}, u32[]{:S(2)}) copy-start(bf16[32,16,32,128]{3,2,0,1:T(8,128)(2,1)} %copy.53) | copy-start | bytes 12582916
  296.9 6.1 %copy-start.8 = (bf16[16,32,32,128]{3,2,1,0:T(8,128)(2,1)S(1)}, bf16[16,32,32,128]{3,2,1,0:T(8,128)(2,1)}, u32[]{:S(2)}) copy-start(bf16[16,32,32,128]{3,2,1,0:T(8,128)(2,1)} %copy-done.7) | copy-start | bytes 12582916
  369.4 3.7 collective-permute-start
  413.4 34.2 %slice-start.2 = ((s8[8388608]{0:T(1024)(128)(4,1)}), s8[4194304]{0:T(1024)(128)(4,1)S(1)}, s32[]{:S(2)}) async-start(s8[8388608]{0:T(1024)(128)(4,1)} %bitcast.114), calls=%async_computation.10 | async-start | bytes 8388608
  432.4 15.2 %slice-start.3 = ((s8[8388608]{0:T(1024)(128)(4,1)}), s8[4194304]{0:T(1024)(128)(4,1)S(1)}, s32[]{:S(2)}) async-start(s8[8388608]{0:T(1024)(128)(4,1)} %bitcast.114), calls=%async_computation.11 | async-start | bytes 8388608
  432.4 24.6 %collective-permute-start.1 = (f32[2432,128]{1,0:T(8,128)S(1)}, f32[2432,128]{1,0:T(8,128)S(1)}, u32[]{:S(2)}, u32[]{:S(2)}) collective-permute-start(f32[2432,128]{1,0:T(8,128)S(1)} %bitcast.125), channel_id=1, source_target_pairs={{0,1},{1,0},{2,3},{3,2},{4,5},{5,4},{6,7},{7,6},{8,9},{9,8},{10,11... | collective-permute-start | bytes 3735560 | tf_op jit(solution)/shard_map/ppermute | solution.py:37
  447.6 1.4 copy-start.11

commit v4 on v3

--- a/solution.py
+++ b/solution.py
@@ -25,14 +25,12 @@
     chips = n_ctx // 2
     half = rows // 2
     part = half // chips
-    piece = part // n_dp
     halves = flat.reshape(2, half, width)
     mine = jnp.where(core == 0, halves[0], halves[1])
     other = jnp.where(core == 0, halves[1], halves[0])
     s1 = mine + lax.ppermute(other, "ctx", pairs)
     a = a2a(s1.reshape(chips, part, width), "ctx", groups).sum(0)
-    b = a2a(a.reshape(n_dp, piece, width), "dp").sum(0)
-    c = a2a(jnp.broadcast_to(b[None], (n_dp, piece, width)), "dp").reshape(part, width)
+    c = a2a(jnp.broadcast_to(a[None], (n_dp, part, width)), "dp").sum(0)
     d = a2a(jnp.broadcast_to(c[None], (chips, part, width)), "ctx", groups).reshape(half, width)
     e = lax.ppermute(d, "ctx", pairs)
     return jnp.where(core == 0, jnp.concatenate([d, e]), jnp.concatenate([e, d]))
@@ -70,9 +68,9 @@
     for q in range(q_n):
         wf_q = wf[:, :, q, :]
         first_q = jnp.einsum("ijc,jdr->dirc", value_blocks, wf_q, preferred_element_type=f32).astype(bf16)
-        first_mid = a2a(first_q, "ctx").reshape(all_blocks, r_n, width)
-        mixed_mid = jnp.einsum("ikc,im->mkc", first_mid, w_second, preferred_element_type=f32).astype(bf16)
-        mixed = a2a(mixed_mid.reshape(n_ctx, local_blocks, r_n, width), "ctx")
+        first_mid = a2a(first_q.reshape(n_ctx, local_blocks, r_n * width), "ctx").reshape(all_blocks, r_n * width)
+        mixed_mid = jnp.dot(w_second.T, first_mid, preferred_element_type=f32).astype(bf16)
+        mixed = a2a(mixed_mid.reshape(n_ctx, local_blocks, r_n * width), "ctx").reshape(n_ctx, local_blocks, r_n, width)
         mixed = mixed.reshape(-1, width)
         xq = x5[:, :, q].transpose(1, 0, 2, 3).reshape(-1, width)
         cq = c5[:, :, q].transpose(1, 0, 2, 3).reshape(-1, width)
@@ -88,13 +86,12 @@
         d_hidden = (cq.astype(f32) + jnp.dot(d_act, w_up.T, preferred_element_type=f32)).astype(bf16)
         d_mixed = (d_hidden.astype(f32) * gq).astype(bf16)
         d_gate = d_hidden.astype(f32) * mixed32 * gq * (1.0 - gq)
-        d_mixed_mid = a2a(d_mixed.reshape(n_ctx, local_blocks, r_n, width), "ctx")
-        d_mixed_mid = d_mixed_mid.reshape(all_blocks, r_n, width)
-        d_first_mid = jnp.einsum("mkc,im->ikc", d_mixed_mid, w_second, preferred_element_type=f32).astype(bf16)
-        grad_second = grad_second + jnp.einsum(
-            "ikc,mkc->im", first_mid, d_mixed_mid, preferred_element_type=f32
-        )
-        d_first = a2a(d_first_mid.reshape(n_ctx, local_blocks, r_n, width), "ctx")
+        d_mixed_mid = a2a(d_mixed.reshape(n_ctx, local_blocks, r_n * width), "ctx")
+        d_mixed_mid = d_mixed_mid.reshape(all_blocks, r_n * width)
+        d_first_mid = jnp.dot(w_second, d_mixed_mid, preferred_element_type=f32).astype(bf16)
+        grad_second = grad_second + jnp.dot(first_mid, d_mixed_mid.T, preferred_element_type=f32)
+        d_first = a2a(d_first_mid.reshape(n_ctx, local_blocks, r_n * width), "ctx")
+        d_first = d_first.reshape(n_ctx, local_blocks, r_n, width)
         d_values = d_values + jnp.einsum("dirc,jdr->ijc", d_first, wf_q, preferred_element_type=f32)
         gf_parts.append(jnp.einsum("ijc,dirc->jdr", value_blocks, d_first, preferred_element_type=f32))
         outs.append(out_q.reshape(n_ctx, local_blocks, r_n, width))

time: 471 us -> 479 us (1.017)
  local copies, waits for them, and re-layouts: 72.6 us -> 86.8 us
  blocking collectives: 124 us -> 118 us
    reshape x1 -> x3, local copies, waits for them, and re-layouts: 0.01 us -> 21.1 us  [the longest x2 13.8 us: body(): first_q.reshape(n_ctx, local_blocks, r_n * width)]
    convert_element_type x3 -> x1, local copies, waits for them, and re-layouts: 18.9 us -> 7.83 us  [body(): mixed32 = mixed.astype(f32)]
    unnamed x33 -> x36, local copies, waits for them, and re-layouts: 9.09 us -> 14.6 us
    all_to_all x5 -> x4, blocking collectives: 124 us -> 118 us  [a2a(): return lax.all_to_all(x, axis, 0, 0, tiled=True, axis_index_groups=groups)]
  transfers between devices with their start and end apart: 5 -> 5, of which waited for: 4 -> 4; matrix products, arithmetic and copies ran while one was open for 14% -> 13% of each run, Pallas kernels for 0% -> 0%
where the time goes in v4:
time: 479 us; the launch traced here: 470 us
  blocking collectives  118 us (25%)
  waiting for transfers between devices  114 us (24%)
  matrix products  110 us (23%)
  local copies, waits for them, and re-layouts  86.8 us (18%)
  starting transfers between devices  24.7 us (5%)
  other arithmetic  14.2 us (3%)
    all_to_all x4, blocking collectives, a2a(): return lax.all_to_all(x, axis, 0, 0, tiled=True, axis_index_groups=groups)  118 us
    all_to_all x3, waiting for transfers between devices, a2a(): return lax.all_to_all(x, axis, 0, 0, tiled=True, axis_index_groups=groups)  111 us
    all_to_all x3, starting transfers between devices, a2a(): return lax.all_to_all(x, axis, 0, 0, tiled=True, axis_index_groups=groups)  19.9 us
    dot_general x1, matrix products, body(): jnp.dot(d_act, w_up.T, preferred_element_type=f32)  16.9 us
    unnamed x36, local copies, waits for them, and re-layouts  14.6 us
    reshape x2, local copies, waits for them, and re-layouts, body(): first_q.reshape(n_ctx, local_blocks, r_n * width)  13.8 us
    dot_general x1, matrix products, body(): jnp.dot(cq, w_down.T, preferred_element_type=f32) * silu_slope(pre)  13 us
    dot_general x1, matrix products, body(): pre = jnp.dot(hidden, w_up, preferred_element_type=f32)  10.7 us
  transfers between devices with their start and end apart: 5, of which 4 were waited for; matrix products, arithmetic and copies ran while one was open for 13% of the time, Pallas kernels for 0%

profile of v4, /device:TPU:1, one launch (start us, length us, event | category | flops | bytes accessed | tf_op | source)
XLA Modules:
  0.0 469.8 jit_solution(9262819961077474739)
XLA Ops:
  19.5 7.3 %reshape.100 = bf16[16,32,4096]{2,0,1:T(8,128)(2,1)} reshape(bf16[16,32,32,128]{3,2,0,1:T(8,128)(2,1)} %convert_bitcast_fusion) | data formatting | bytes 8388608 | tf_op jit(solution)/shard_map/reshape | solution.py:71
  26.7 6.5 %copy.39 = bf16[16,32,4096]{2,1,0:T(8,128)(2,1)} copy(bf16[16,32,4096]{2,0,1:T(8,128)(2,1)} %reshape.100) | data formatting | bytes 8388608 | tf_op jit(solution)/shard_map/reshape | solution.py:71
  33.2 8.4 %all-to-all-start = ((bf16[16,32,4096]{2,1,0:T(8,128)(2,1)}), bf16[16,32,4096]{2,1,0:T(8,128)(2,1)}, u32[]{:S(2)}, u32[]{:S(2)}) async-start(bf16[16,32,4096]{2,1,0:T(8,128)(2,1)} %copy.39), calls=%async_computation | async-start | bytes 8388608 | tf_op jit(solution)/shard_map/all_to_all | solution.py:15
  51.6 41.0 %all-to-all-done = bf16[16,32,4096]{2,1,0:T(8,128)(2,1)} async-done(((bf16[16,32,4096]{2,1,0:T(8,128)(2,1)}), bf16[16,32,4096]{2,1,0:T(8,128)(2,1)}, u32[]{:S(2)}, u32[]{:S(2)}) %all-to-all-start) | async-done | bytes 4194336 | tf_op jit(solution)/shard_map/all_to_all | solution.py:15
  92.6 6.6 %convolution_convert_fusion.1 = bf16[4096,512]{0,1:T(8,128)(2,1)} fusion(bf16[512,4096]{1,0:T(8,128)(2,1)} %bitcast.13, bf16[512,512]{1,0:T(8,128)(2,1)S(1)} %copy-done), kind=kOutput, calls=%fused_computation.29 | convolution fusion | flops 2149580800 | bytes 8912896 | tf_op jit(solution)/shard_map/dot_general | solution.py:72
  99.2 5.9 %all-to-all-start.1 = ((bf16[16,32,4096]{2,1,0:T(8,128)(2,1)}), bf16[16,32,4096]{2,1,0:T(8,128)(2,1)}, u32[]{:S(2)}, u32[]{:S(2)}) async-start(bf16[16,32,4096]{2,1,0:T(8,128)(2,1)} %bitcast.159), calls=%async_computation.1 | async-start | bytes 8388608 | tf_op jit(solution)/shard_map/all_to_all | solution.py:15
  114.0 42.0 %all-to-all-done.1 = bf16[16,32,4096]{2,1,0:T(8,128)(2,1)} async-done(((bf16[16,32,4096]{2,1,0:T(8,128)(2,1)}), bf16[16,32,4096]{2,1,0:T(8,128)(2,1)}, u32[]{:S(2)}, u32[]{:S(2)}) %all-to-all-start.1) | async-done | bytes 4194336 | tf_op jit(solution)/shard_map/all_to_all | solution.py:15
  156.0 7.8 %reshape.120 = f32[16384,128]{1,0:T(8,128)} reshape(bf16[16,32,4096]{2,1,0:T(8,128)(2,1)} %all-to-all-done.1) | data formatting | bytes 12582912 | tf_op jit(solution)/shard_map/convert_element_type | solution.py:78
  163.8 8.9 %fusion.9 = bf16[16384,128]{1,0:T(8,128)(2,1)S(1)} fusion(f32[32,16,32,128]{3,2,0,1:T(8,128)} %copy.36, f32[16384,128]{1,0:T(8,128)} %reshape.120, f32[16,32,32,128]{3,2,1,0:T(8,128)} %copy.37), kind=kLoop, calls=%fused_computation.20 | loop fusion | flops 6291456 | bytes 29360128 | tf_op jit(solution)/shard_map/convert_element_type | solution.py:79
  172.7 10.7 %multiply_convert_fusion = (bf16[16384,256]{1,0:T(8,128)(2,1)}, f32[16384,256]{1,0:T(8,128)}) fusion(bf16[16384,128]{1,0:T(8,128)(2,1)S(1)} %fusion.9, bf16[128,256]{1,0:T(8,128)(2,1)S(1)} %copy-done.12), kind=kOutput, calls=%fused_computation.10 | convolution fusion | flops 1094713344 | bytes 29425664 | tf_op jit(solution)/shard_map/dot_general | solution.py:80
  183.4 13.0 %fusion = bf16[16384,256]{1,0:T(8,128)(2,1)} fusion(bf16[16384,128]{1,0:T(8,128)(2,1)S(1)} %bitcast.132, bf16[256,128]{1,0:T(8,128)(2,1)S(1)} %copy-done.13, f32[16384,256]{1,0:T(8,128)} %get-tuple-element.15), kind=kOutput, calls=%fused_computation.1 | convolution fusion | flops 1111490560 | bytes 29425664 | tf_op jit(solution)/shard_map/dot_general | solution.py:84
  196.4 16.9 %fusion.11 = (bf16[16384,128]{1,0:T(8,128)(2,1)}, bf16[16384,128]{1,0:T(8,128)(2,1)}, f32[16384,128]{1,0:T(8,128)}) fusion(f32[16,32,32,128]{3,2,1,0:T(8,128)} %copy.37, f32[16384,128]{1,0:T(8,128)} %reshape.120, bf16[16384,256]{1,0:T(8,128)(2,1)} %fusion, bf16[128,256]{1,0:T(8,128)(2,1)S(1)} %copy-done.12, bf16[16384,128]{1,0:T(8,128)(2,1)S(1)} %bitcast.133), kind=kOutput, calls=%fused_computation.26 | convolution fusion | flops 1096810496 | bytes 46202880 | tf_op jit(solution)/shard_map/dot_general | solution.py:86
  213.3 7.3 %reshape.105 = bf16[16,32,4096]{2,1,0:T(8,128)(2,1)} reshape(bf16[16384,128]{1,0:T(8,128)(2,1)} %get-tuple-element.8) | data formatting | bytes 8388608 | tf_op jit(solution)/shard_map/reshape | solution.py:89
  220.6 55.3 %all_to_all.35 = bf16[16,32,4096]{2,1,0:T(8,128)(2,1)S(1)} all-to-all(bf16[16,32,4096]{2,1,0:T(8,128)(2,1)} %reshape.105), channel_id=1, replica_groups=mesh['dp'=8,'ctx'=16] {'ctx'}, dimensions={0} | all-to-all | bytes 8388608 | tf_op jit(solution)/shard_map/all_to_all | solution.py:15
  285.8 6.2 %fusion.37 = f32[128,256]{1,0:T(8,128)S(1)} fusion(bf16[16384,128]{1,0:T(8,128)(2,1)} %copy-done.4, bf16[16384,256]{1,0:T(8,128)(2,1)} %fusion), kind=kOutput, calls=%fused_computation.55 | convolution fusion | flops 1073741824 | bytes 12713984 | tf_op jit(solution)/shard_map/dot_general | solution.py:85
  297.6 6.1 %fusion.38 = f32[256,128]{1,0:T(8,128)S(1)} fusion(bf16[16384,256]{1,0:T(8,128)(2,1)} %get-tuple-element.14, bf16[16384,128]{1,0:T(8,128)(2,1)S(1)} %bitcast.134), kind=kOutput, calls=%fused_computation.56 | convolution fusion | flops 1073741824 | bytes 12713984 | tf_op jit(solution)/shard_map/dot_general | solution.py:83
  308.3 28.5 %all-to-all-done.3 = bf16[16,32,4096]{2,1,0:T(8,128)(2,1)} async-done(((bf16[16,32,4096]{2,1,0:T(8,128)(2,1)}), bf16[16,32,4096]{2,1,0:T(8,128)(2,1)}, u32[]{:S(2)}, u32[]{:S(2)}) %all-to-all-start.3) | async-done | bytes 4194336 | tf_op jit(solution)/shard_map/all_to_all | solution.py:15
  347.4 6.6 %copy.45 = bf16[32,512,128]{2,1,0:T(8,128)(2,1)} copy(bf16[32,512,128]{1,2,0:T(8,128)(2,1)} %fusion.14) | data formatting | bytes 8388608 | tf_op jit(solution)/shard_map/dirc,jdr->ijc/transpose | solution.py:95
  354.0 7.0 %fusion.28 = f32[128,256]{0,1:T(8,128)S(1)} fusion(bf16[1,16384,128]{2,1,0:T(8,128)(2,1)} %param.7, bf16[16384,128]{1,0:T(8,128)(2,1)} %bitcast.151, bf16[16384,128]{1,0:T(8,128)(2,1)} %bitcast.149), kind=kOutput, calls=%fused_computation.48 | convolution fusion | flops 1090519040 | bytes 12713984 | tf_op jit(solution)/shard_map/dot_general | solution.py:109
  378.0 21.3 %all_to_all.36 = f32[8,304,128]{2,1,0:T(8,128)S(1)} all-to-all(f32[8,304,128]{2,1,0:T(8,128)S(1)} %bitcast.145), channel_id=1, replica_groups={{0,2,4,6,8,10,12,14},{1,3,5,7,9,11,13,15},{16,18,20,22,24,26,28,30},{17..., dimensions={0} | all-to-all | bytes 2490368 | tf_op jit(solution)/shard_map/all_to_all | solution.py:15
  399.4 20.7 %all_to_all.37 = f32[8,304,128]{2,1,0:T(8,128)S(1)} all-to-all(f32[8,304,128]{2,1,0:T(8,128)S(1)} %broadcast_in_dim.7), channel_id=1, replica_groups=mesh['dp'=8,'ctx'=16] {'dp'}, dimensions={0} | all-to-all | bytes 2490368 | tf_op jit(solution)/shard_map/all_to_all | solution.py:15
  420.3 21.1 %all_to_all.38 = f32[8,304,128]{2,1,0:T(8,128)S(1)} all-to-all(f32[8,304,128]{2,1,0:T(8,128)S(1)} %broadcast_in_dim.8), channel_id=1, replica_groups={{0,2,4,6,8,10,12,14},{1,3,5,7,9,11,13,15},{16,18,20,22,24,26,28,30},{17..., dimensions={0} | all-to-all | bytes 2490368 | tf_op jit(solution)/shard_map/all_to_all | solution.py:15
  445.1 6.9 %fusion.1 = bf16[16384,128]{1,0:T(8,128)(2,1)S(1)} fusion(bf16[16384,256]{1,0:T(8,128)(2,1)} %get-tuple-element.14, bf16[256,128]{1,0:T(8,128)(2,1)S(1)} %copy-done.13, bf16[16384,128]{1,0:T(8,128)(2,1)} %copy-done.4), kind=kOutput, calls=%fused_computation.5 | convolution fusion | flops 1080033280 | bytes 16842752 | tf_op jit(solution)/shard_map/dot_general | solution.py:82
  456.7 7.9 %fusion.5 = bf16[1,16384,128]{2,1,0:T(8,128)(2,1)} fusion(f32[16384,128]{1,0:T(8,128)S(1)} %bitcast.142, bf16[128,256]{1,0:T(8,128)(2,1)S(1)} %copy-done.14, bf16[16384,128]{1,0:T(8,128)(2,1)} %bitcast.152, bf16[16384,128]{1,0:T(8,128)(2,1)} %bitcast.150), kind=kOutput, calls=%fused_computation.9 | convolution fusion | flops 1094713344 | bytes 21037056 | tf_op jit(solution)/shard_map/dot_general | solution.py:111
  (75 shorter events, 98.5 us)
Async XLA Ops:
  0.6 92.0 %copy-start = (bf16[512,512]{1,0:T(8,128)(2,1)S(1)}, bf16[512,512]{1,0:T(8,128)(2,1)}, u32[]{:S(2)}) copy-start(bf16[512,512]{1,0:T(8,128)(2,1)} %param.11) | copy-start | bytes 1572868
  2.0 11.0 %copy-start.10 = (bf16[512,512]{0,1:T(8,128)(2,1)}, bf16[512,512]{0,1:T(8,128)(2,1)S(1)}, u32[]{:S(2)}) copy-start(bf16[512,512]{0,1:T(8,128)(2,1)S(1)} %copy.38) | copy-start | bytes 1572868
  6.7 5.7 %copy-start.1 = (f32[16384,256]{1,0:T(8,128)}, f32[16384,256]{1,0:T(8,128)S(1)}, u32[]{:S(2)}) copy-start(f32[16384,256]{1,0:T(8,128)S(1)} %fusion.20) | copy-start | bytes 50331652
  13.0 2.1 copy-start.6
  33.2 59.3 %all-to-all-start = ((bf16[16,32,4096]{2,1,0:T(8,128)(2,1)}), bf16[16,32,4096]{2,1,0:T(8,128)(2,1)}, u32[]{:S(2)}, u32[]{:S(2)}) async-start(bf16[16,32,4096]{2,1,0:T(8,128)(2,1)} %copy.39), calls=%async_computation | async-start | bytes 8388608 | tf_op jit(solution)/shard_map/all_to_all | solution.py:15
  41.7 5.5 %copy-start.5 = (bf16[1,16384,128]{2,1,0:T(8,128)(2,1)S(1)}, bf16[1,16384,128]{2,1,0:T(8,128)(2,1)}, u32[]{:S(2)}) copy-start(bf16[1,16384,128]{2,1,0:T(8,128)(2,1)} %param.7) | copy-start | bytes 12582916
  99.2 56.8 %all-to-all-start.1 = ((bf16[16,32,4096]{2,1,0:T(8,128)(2,1)}), bf16[16,32,4096]{2,1,0:T(8,128)(2,1)}, u32[]{:S(2)}, u32[]{:S(2)}) async-start(bf16[16,32,4096]{2,1,0:T(8,128)(2,1)} %bitcast.159), calls=%async_computation.1 | async-start | bytes 8388608 | tf_op jit(solution)/shard_map/all_to_all | solution.py:15
  163.8 8.9 %copy-start.12 = (bf16[128,256]{1,0:T(8,128)(2,1)S(1)}, bf16[128,256]{1,0:T(8,128)(2,1)}, u32[]{:S(2)}) copy-start(bf16[128,256]{1,0:T(8,128)(2,1)} %param.12) | copy-start | bytes 196612
  172.7 10.7 %copy-start.4 = (bf16[16384,128]{1,0:T(8,128)(2,1)}, bf16[16384,128]{1,0:T(8,128)(2,1)S(1)}, u32[]{:S(2)}) copy-start(bf16[16384,128]{1,0:T(8,128)(2,1)S(1)} %fusion.9) | copy-start | bytes 12582916
  172.7 10.7 %copy-start.2 = (bf16[32,16,32,128]{3,2,0,1:T(8,128)(2,1)S(1)}, bf16[32,16,32,128]{3,2,0,1:T(8,128)(2,1)}, u32[]{:S(2)}) copy-start(bf16[32,16,32,128]{3,2,0,1:T(8,128)(2,1)} %copy.41) | copy-start | bytes 12582916
  172.7 10.7 %copy-start.13 = (bf16[256,128]{1,0:T(8,128)(2,1)S(1)}, bf16[256,128]{1,0:T(8,128)(2,1)}, u32[]{:S(2)}) copy-start(bf16[256,128]{1,0:T(8,128)(2,1)} %param.13) | copy-start | bytes 196612
  275.9 4.3 copy-start.7
  280.2 56.6 %all-to-all-start.3 = ((bf16[16,32,4096]{2,1,0:T(8,128)(2,1)}), bf16[16,32,4096]{2,1,0:T(8,128)(2,1)}, u32[]{:S(2)}, u32[]{:S(2)}) async-start(bf16[16,32,4096]{2,1,0:T(8,128)(2,1)} %bitcast.153), calls=%async_computation.3 | async-start | bytes 8388608 | tf_op jit(solution)/shard_map/all_to_all | solution.py:15
  292.0 5.6 %copy-start.3 = (bf16[32,16,32,128]{3,2,0,1:T(8,128)(2,1)S(1)}, bf16[32,16,32,128]{3,2,0,1:T(8,128)(2,1)}, u32[]{:S(2)}) copy-start(bf16[32,16,32,128]{3,2,0,1:T(8,128)(2,1)} %copy.41) | copy-start | bytes 12582916
  297.6 6.1 %copy-start.8 = (bf16[16,32,4096]{2,1,0:T(8,128)(2,1)S(1)}, bf16[16,32,4096]{2,1,0:T(8,128)(2,1)}, u32[]{:S(2)}) copy-start(bf16[16,32,4096]{2,1,0:T(8,128)(2,1)} %copy-done.7) | copy-start | bytes 12582916
  336.8 5.5 %copy-start.11 = (bf16[512,512]{0,1:T(8,128)(2,1)S(1)}, bf16[512,512]{0,1:T(8,128)(2,1)}, u32[]{:S(2)}) copy-start(bf16[512,512]{0,1:T(8,128)(2,1)} %copy-done.10) | copy-start | bytes 1572868
  340.3 2.0 copy-start.9
  374.2 3.7 collective-permute-start
  420.2 35.0 %slice-start = ((s8[8388608]{0:T(1024)(128)(4,1)}), s8[4194304]{0:T(1024)(128)(4,1)S(1)}, s32[]{:S(2)}) async-start(s8[8388608]{0:T(1024)(128)(4,1)} %bitcast.135), calls=%async_computation.7 | async-start | bytes 8388608
  441.4 13.8 %slice-start.1 = ((s8[8388608]{0:T(1024)(128)(4,1)}), s8[4194304]{0:T(1024)(128)(4,1)S(1)}, s32[]{:S(2)}) async-start(s8[8388608]{0:T(1024)(128)(4,1)} %bitcast.135), calls=%async_computation.8 | async-start | bytes 8388608
  441.4 23.2 %collective-permute-start.1 = (f32[2432,128]{1,0:T(8,128)S(1)}, f32[2432,128]{1,0:T(8,128)S(1)}, u32[]{:S(2)}, u32[]{:S(2)}) collective-permute-start(f32[2432,128]{1,0:T(8,128)S(1)} %bitcast.143), channel_id=1, source_target_pairs={{0,1},{1,0},{2,3},{3,2},{4,5},{5,4},{6,7},{7,6},{8,9},{9,8},{10,11... | collective-permute-start | bytes 3735560 | tf_op jit(solution)/shard_map/ppermute | solution.py:35
  455.2 1.4 copy-start.14
